TPU v7x, 256 devices: a whole 4x4x8 slice. The times are simulated.
256 devices in a mesh: row: 16 (over z, core), col: 16 (over x, y).
Axes of the slice: x: 4, y: 4, z: 8, core: 2. Of those that a mesh axis runs over, the one named last changes fastest.
Arguments:
- site_tensor: bfloat16 [1024, 4, 1024], P('row', None, 'col'), may hold values from -180 to 180
- site_tangent: bfloat16 [1024, 4, 1024], P('row', None, 'col'), may hold values from -180 to 180
- left_env: bfloat16 [1024, 16384], P('row', 'col'), may hold values from -0.1875 to 0.375
- right_env: bfloat16 [1024, 16384], P('row', 'col'), may hold values from -0.046875 to 0.09375
- mpo: bfloat16 [16, 16, 4, 4], replicated, may hold values from -0.25 to 0.75
- dissipation: float32 [4], replicated, may hold values from 0.2 to 2
Outputs:
- evolved: float32 [1024, 4, 1024], P('row', None, 'col')
- evolved_tangent: float32 [1024, 4, 1024], P('row', None, 'col')
All inputs are finite; a program needn't handle non-finite values.
Results may differ from a plain program's by a relative error of at most 0.0055.
Values may be sent and summed in bfloat16 or wider, within the bound.
No kernel may reach another device: no remote copies, remote signals or barrier semaphores. Data moves between devices by JAX's collectives and lax.ppermute only.
A program may use at most 64 MiB of HBM per device.

v0:
```python
import jax
import jax.numpy as jnp
from jax import lax
from jax.sharding import PartitionSpec as P

KRYLOV = 3


taylor_order = 16


def inner(first, second):
    return jnp.sum(first * second)


def taylor(hess, dhess):
    size = hess.shape[0]
    term = jnp.zeros((size,), jnp.float32).at[0].set(1.0)
    dterm = jnp.zeros((size,), jnp.float32)
    total = term
    dtotal = dterm
    for order in range(1, taylor_order + 1):
        nterm = jnp.dot(hess, term, precision=lax.Precision.HIGHEST) / order
        dterm = (
            jnp.dot(dhess, term, precision=lax.Precision.HIGHEST)
            + jnp.dot(hess, dterm, precision=lax.Precision.HIGHEST)
        ) / order
        term = nterm
        total = total + term
        dtotal = dtotal + dterm
    return (total, dtotal)


def local(site_tensor, site_tangent, left_env, right_env, mpo, dissipation):
    rows_here, physical, cols_here = site_tensor.shape
    channels = mpo.shape[0]
    left_whole = lax.all_gather(left_env, "col", axis=1, tiled=True)
    right_whole = lax.all_gather(right_env, "row", axis=0, tiled=True)

    def apply(stacked):
        panels = stacked.shape[1]
        whole = lax.all_gather(stacked.astype(jnp.bfloat16), "row", axis=0, tiled=True)
        flat = whole.reshape(whole.shape[0], panels * physical * cols_here)
        left_three = left_whole.reshape(rows_here, flat.shape[0], channels)
        mixed = lax.dot_general(
            left_three, flat, (((1,), (0,)), ((), ())), preferred_element_type=jnp.float32
        )
        mixed = mixed.astype(jnp.bfloat16).reshape(rows_here, channels, panels, physical, cols_here)
        channel = jnp.einsum("awspr,wvpq->asqrv", mixed, mpo, preferred_element_type=jnp.float32)
        channel = channel.astype(jnp.bfloat16).reshape(
            rows_here * panels * physical, cols_here * channels
        )
        partial_rows = lax.dot_general(
            channel, right_whole, (((1,), (1,)), ((), ())), preferred_element_type=jnp.float32
        )
        partial_rows = partial_rows.reshape(rows_here, panels, physical, partial_rows.shape[1])
        summed = lax.psum_scatter(partial_rows, "col", scatter_dimension=3, tiled=True)
        return summed - dissipation[None, None, :, None] * stacked

    primal = site_tensor.astype(jnp.float32)
    tangent = site_tangent.astype(jnp.float32)
    starting = lax.psum(jnp.stack([inner(primal, primal), inner(primal, tangent)]), ("row", "col"))
    norm_site = jnp.sqrt(starting[0])
    norm_tangent = starting[1] / norm_site
    basis = [primal / norm_site]
    tangents = [(tangent - basis[0] * norm_tangent) / norm_site]
    hess = jnp.zeros((KRYLOV, KRYLOV), jnp.float32)
    dhess = jnp.zeros((KRYLOV, KRYLOV), jnp.float32)
    for level in range(KRYLOV):
        image = apply(basis[level][:, None])[:, 0]
        dimage = apply(tangents[level][:, None])[:, 0]
        counted = level + 1
        locals_list = [inner(vector, image) for vector in basis]
        locals_list = locals_list + [inner(vector, image) for vector in tangents]
        locals_list = locals_list + [inner(vector, dimage) for vector in basis]
        totals = lax.psum(jnp.stack(locals_list), ("row", "col"))
        coeffs = totals[:counted]
        across = totals[counted : 2 * counted]
        along = totals[2 * counted : 3 * counted]
        dcoeffs = across + along
        hess = hess.at[:counted, level].set(coeffs)
        dhess = dhess.at[:counted, level].set(dcoeffs)
        if level + 1 < KRYLOV:
            residual = image
            dresidual = dimage
            for index in range(counted):
                residual = residual - coeffs[index] * basis[index]
                dresidual = (
                    dresidual - dcoeffs[index] * basis[index] - coeffs[index] * tangents[index]
                )
            paired = lax.psum(
                jnp.stack([inner(residual, residual), inner(residual, dresidual)]), ("row", "col")
            )
            squared = paired[0]
            mixed_term = paired[1]
            height = jnp.sqrt(squared)
            dheight = mixed_term / height
            newvec = residual / height
            basis.append(newvec)
            tangents.append((dresidual - newvec * dheight) / height)
            hess = hess.at[level + 1, level].set(height)
            dhess = dhess.at[level + 1, level].set(dheight)
    coeff, dcoeff = taylor(hess, dhess)
    spread = jnp.zeros_like(primal)
    dspread = jnp.zeros_like(primal)
    for index in range(KRYLOV):
        spread = spread + coeff[index] * basis[index]
        dspread = dspread + coeff[index] * tangents[index] + dcoeff[index] * basis[index]
    evolved = norm_site * spread
    evolved_tangent = norm_tangent * spread + norm_site * dspread
    return (evolved, evolved_tangent)


def solution(mesh):
    in_specs = (
        P("row", None, "col"),
        P("row", None, "col"),
        P("row", "col"),
        P("row", "col"),
        P(),
        P(),
    )
    out_specs = (P("row", None, "col"), P("row", None, "col"))
    return jax.shard_map(local, mesh=mesh, in_specs=in_specs, out_specs=out_specs, check_vma=False)
```

profile of v0, /device:TPU:1, one launch (start us, length us, event | category | flops | bytes accessed | tf_op | source)
XLA Modules:
  0.0 1113.4 jit_solution(7619003044250572234)
XLA Ops:
  11.6 81.9 %psum.42 = f32[2]{0:T(128)S(1)} all-reduce(f32[2]{0:T(128)S(1)} %pad_maximum_fusion), channel_id=1, replica_groups=mesh['row'=16,'col'=16] {'row','col'}, use_global_device_ids=true, to_apply=%region_2.0 | all-reduce | flops 2 | bytes 16 | tf_op jit(solution)/shard_map/psum | solution.py:62
  96.4 18.8 %all-gather = bf16[1024,4,64]{2,1,0:T(4,128)(2,1)S(1)} all-gather(bf16[64,4,64]{2,1,0:T(4,128)(2,1)S(1)} %get-tuple-element.182), channel_id=2, replica_groups=mesh['row'=16,'col'=16] {'row'}, dimensions={0}, use_global_device_ids=true | all-gather | bytes 557056 | tf_op jit(solution)/shard_map/all_gather | solution.py:42
  116.0 4.8 copy.120
  120.8 4.5 copy.122
  137.6 18.6 %all-gather.1 = bf16[1024,4,64]{2,1,0:T(4,128)(2,1)S(1)} all-gather(bf16[64,4,64]{2,1,0:T(4,128)(2,1)S(1)} %get-tuple-element.181), channel_id=3, replica_groups=mesh['row'=16,'col'=16] {'row'}, dimensions={0}, use_global_device_ids=true | all-gather | bytes 557056 | tf_op jit(solution)/shard_map/all_gather | solution.py:42
  161.8 3.6 copy.133
  173.1 37.3 %reduce-scatter.19.cloned.1.call-done = f32[64,256]{1,0:T(8,128)} async-done(((f32[1024,256]{1,0:T(8,128)}), f32[64,256]{1,0:T(8,128)}) %reduce-scatter.19.cloned.1.call-update) | async-done | bytes 65552
  211.4 80.8 %reduce-scatter.21.cloned.1.call-done = f32[64,256]{1,0:T(8,128)} async-done(((f32[1024,256]{1,0:T(8,128)}), f32[64,256]{1,0:T(8,128)}) %reduce-scatter.21.cloned.1.call-update) | async-done | bytes 65552
  296.1 77.2 %psum.43 = f32[3]{0:T(128)S(1)} all-reduce(f32[3]{0:T(128)S(1)} %pad_maximum_fusion.1), channel_id=1, replica_groups=mesh['row'=16,'col'=16] {'row','col'}, use_global_device_ids=true, to_apply=%region_8.0 | all-reduce | flops 3 | bytes 24 | tf_op jit(solution)/shard_map/psum | solution.py:76
  378.1 73.2 %psum.44 = f32[2]{0:T(128)S(1)} all-reduce(f32[2]{0:T(128)S(1)} %pad_maximum_fusion.2), channel_id=1, replica_groups=mesh['row'=16,'col'=16] {'row','col'}, use_global_device_ids=true, to_apply=%region_11.0 | all-reduce | flops 2 | bytes 16 | tf_op jit(solution)/shard_map/psum | solution.py:91
  453.9 18.9 %all-gather.2 = bf16[1024,4,64]{2,1,0:T(4,128)(2,1)S(1)} all-gather(bf16[64,4,64]{2,1,0:T(4,128)(2,1)S(1)} %get-tuple-element.180), channel_id=4, replica_groups=mesh['row'=16,'col'=16] {'row'}, dimensions={0}, use_global_device_ids=true | all-gather | bytes 557056 | tf_op jit(solution)/shard_map/all_gather | solution.py:42
  474.1 3.3 fusion.38
  482.2 3.6 copy.141
  493.5 18.4 %all-gather.3 = bf16[1024,4,64]{2,1,0:T(4,128)(2,1)S(1)} all-gather(bf16[64,4,64]{2,1,0:T(4,128)(2,1)} %get-tuple-element.173), channel_id=5, replica_groups=mesh['row'=16,'col'=16] {'row'}, dimensions={0}, use_global_device_ids=true | all-gather | bytes 557056 | tf_op jit(solution)/shard_map/all_gather | solution.py:42
  513.3 3.3 fusion.39
  521.4 3.6 copy.149
  532.6 33.9 %reduce-scatter.23.cloned.1.call-done = f32[64,256]{1,0:T(8,128)} async-done(((f32[1024,256]{1,0:T(8,128)}), f32[64,256]{1,0:T(8,128)}) %reduce-scatter.23.cloned.1.call-update) | async-done | bytes 65552
  567.6 80.8 %reduce-scatter.25.cloned.1.call-done = f32[64,256]{1,0:T(8,128)} async-done(((f32[1024,256]{1,0:T(8,128)}), f32[64,256]{1,0:T(8,128)}) %reduce-scatter.25.cloned.1.call-update) | async-done | bytes 65552
  650.4 3.9 stack.106
  654.3 77.2 %psum.45 = f32[6]{0:T(128)S(1)} all-reduce(f32[6]{0:T(128)S(1)} %stack.106), channel_id=1, replica_groups=mesh['row'=16,'col'=16] {'row','col'}, use_global_device_ids=true, to_apply=%region_20.0 | all-reduce | flops 6 | bytes 48 | tf_op jit(solution)/shard_map/psum | solution.py:76
  732.8 3.4 multiply_reduce_fusion.1
  737.5 73.3 %psum.46 = f32[2]{0:T(128)S(1)} all-reduce(f32[2]{0:T(128)S(1)} %pad_maximum_fusion.3), channel_id=1, replica_groups=mesh['row'=16,'col'=16] {'row','col'}, use_global_device_ids=true, to_apply=%region_23.0 | all-reduce | flops 2 | bytes 16 | tf_op jit(solution)/shard_map/psum | solution.py:91
  813.4 18.9 %all-gather.5 = bf16[1024,4,64]{2,1,0:T(4,128)(2,1)S(1)} all-gather(bf16[64,4,64]{2,1,0:T(4,128)(2,1)S(1)} %get-tuple-element.168), channel_id=7, replica_groups=mesh['row'=16,'col'=16] {'row'}, dimensions={0}, use_global_device_ids=true | all-gather | bytes 557056 | tf_op jit(solution)/shard_map/all_gather | solution.py:42
  841.8 3.6 copy.165
  853.1 18.5 %all-gather.4 = bf16[1024,4,64]{2,1,0:T(4,128)(2,1)S(1)} all-gather(bf16[64,4,64]{2,1,0:T(4,128)(2,1)} %get-tuple-element.179), channel_id=6, replica_groups=mesh['row'=16,'col'=16] {'row'}, dimensions={0}, use_global_device_ids=true | all-gather | bytes 557056 | tf_op jit(solution)/shard_map/all_gather | solution.py:42
  872.9 3.3 fusion.40
  881.1 3.6 copy.157
  894.8 31.1 %reduce-scatter.29.cloned.1.call-done = f32[64,256]{1,0:T(8,128)} async-done(((f32[1024,256]{1,0:T(8,128)}), f32[64,256]{1,0:T(8,128)}) %reduce-scatter.29.cloned.1.call-update) | async-done | bytes 65552
  927.0 80.9 %reduce-scatter.27.cloned.1.call-done = f32[64,256]{1,0:T(8,128)} async-done(((f32[1024,256]{1,0:T(8,128)}), f32[64,256]{1,0:T(8,128)}) %reduce-scatter.27.cloned.1.call-update) | async-done | bytes 65552
  1010.3 5.8 stack.119
  1016.2 77.2 %psum.47 = f32[9]{0:T(128)S(1)} all-reduce(f32[9]{0:T(128)S(1)} %stack.119), channel_id=1, replica_groups=mesh['row'=16,'col'=16] {'row','col'}, use_global_device_ids=true, to_apply=%region_35.0 | all-reduce | flops 9 | bytes 72 | tf_op jit(solution)/shard_map/psum | solution.py:76
  1101.5 4.5 multiply_add_fusion
  (179 shorter events, 121.0 us)
Async XLA Ops:
  7.2 108.7 %copy-start.8 = (bf16[16,16,4,4]{1,3,2,0:T(4,128)(2,1)S(1)}, bf16[16,16,4,4]{1,3,2,0:T(4,128)(2,1)}, u32[]{:S(2)}) copy-start(bf16[16,16,4,4]{1,3,2,0:T(4,128)(2,1)} %param.32) | copy-start | bytes 24580
  7.2 108.9 %all-gather.9.cloned.1.call-start = ((), (), s32[]{:S(2)}) async-start(), calls=%async_computation.6 | async-start | bytes 2228224 | tf_op jit(solution)/shard_map/all_gather | solution.py:37
  7.9 123.7 %all-gather.11.cloned.1.call-start = ((), (), s32[]{:S(2)}) async-start(), calls=%async_computation.7 | async-start | bytes 2228224 | tf_op jit(solution)/shard_map/all_gather | solution.py:38
  8.7 201.7 %reduce-scatter.19.cloned.1.call-start = ((), (), s32[]{:S(2)}) async-start(), calls=%async_computation.8 | async-start | bytes 1114112
  116.0 43.8 %copy-start.9 = (bf16[16,16,4,4]{0,1,2,3:T(8,128)(2,1)}, bf16[16,16,4,4]{0,1,2,3:T(8,128)(2,1)S(1)}, u32[]{:S(2)}) copy-start(bf16[16,16,4,4]{0,1,2,3:T(8,128)(2,1)S(1)} %copy.124) | copy-start | bytes 24580
  125.3 3.6 copy-start.5
  137.6 20.1 %copy-start.6 = (bf16[64,1024,16]{1,0,2:T(8,128)(2,1)S(1)}, bf16[64,1024,16]{1,0,2:T(8,128)(2,1)}, u32[]{:S(2)}) copy-start(bf16[64,1024,16]{1,0,2:T(8,128)(2,1)} %copy-done.5) | copy-start | bytes 6291460
  137.6 154.6 %reduce-scatter.21.cloned.1.call-start = ((), (), s32[]{:S(2)}) async-start(), calls=%async_computation.9 | async-start | bytes 1114112
  159.9 5.6 copy-start
  169.7 123.6 %copy-start.1 = (bf16[64,4,64]{2,1,0:T(4,128)(2,1)S(1)}, bf16[64,4,64]{2,1,0:T(4,128)(2,1)}, u32[]{:S(2)}) copy-start(bf16[64,4,64]{2,1,0:T(4,128)(2,1)} %param.28) | copy-start | bytes 98308
  169.7 123.6 %copy-start.2 = (bf16[64,4,64]{2,1,0:T(4,128)(2,1)S(1)}, bf16[64,4,64]{2,1,0:T(4,128)(2,1)}, u32[]{:S(2)}) copy-start(bf16[64,4,64]{2,1,0:T(4,128)(2,1)} %param.29) | copy-start | bytes 98308
  169.7 123.6 %copy-start.10 = (f32[4]{0:T(128)S(1)}, f32[4]{0:T(128)}, u32[]{:S(2)}) copy-start(f32[4]{0:T(128)} %param.33) | copy-start | bytes 52
  173.0 393.5 %reduce-scatter.23.cloned.1.call-start = ((), (), s32[]{:S(2)}) async-start(), calls=%async_computation.10 | async-start | bytes 1114112
  493.4 154.9 %reduce-scatter.25.cloned.1.call-start = ((), (), s32[]{:S(2)}) async-start(), calls=%async_computation.11 | async-start | bytes 1114112
  532.6 393.4 %reduce-scatter.29.cloned.1.call-start = ((), (), s32[]{:S(2)}) async-start(), calls=%async_computation.13 | async-start | bytes 1114112
  736.2 77.2 %copy-start.3 = (f32[64,4,64]{2,1,0:T(4,128)}, f32[64,4,64]{2,1,0:T(4,128)S(1)}, u32[]{:S(2)}) copy-start(f32[64,4,64]{2,1,0:T(4,128)S(1)} %get-tuple-element.171) | copy-start | bytes 196612
  853.0 155.0 %reduce-scatter.27.cloned.1.call-start = ((), (), s32[]{:S(2)}) async-start(), calls=%async_computation.12 | async-start | bytes 1114112
  888.2 120.9 %copy-start.4 = (f32[64,4,64]{2,1,0:T(4,128)S(1)}, f32[64,4,64]{2,1,0:T(4,128)}, u32[]{:S(2)}) copy-start(f32[64,4,64]{2,1,0:T(4,128)} %copy-done.3) | copy-start | bytes 196612
  888.2 120.9 %copy-start.7 = (f32[64,4,64]{2,1,0:T(4,128)S(1)}, f32[64,4,64]{2,1,0:T(4,128)}, u32[]{:S(2)}) copy-start(f32[64,4,64]{2,1,0:T(4,128)} %get-tuple-element.169) | copy-start | bytes 196612
  890.3 203.3 %copy-start.11 = (f32[3,1]{0,1:T(1,128)S(1)}, f32[3,1]{0,1:T(1,128)}, u32[]{:S(2)}) copy-start(f32[3,1]{0,1:T(1,128)} %constant.327) | copy-start | bytes 40
Sparse Core Ops, SparseCore 0:
  10.5 52.1 all-gather.8
  64.5 40.9 all-gather.10
  137.7 72.6 reduce-scatter.18
  213.7 78.4 reduce-scatter.20
  493.6 72.8 reduce-scatter.22
  569.8 78.4 reduce-scatter.24
  853.1 72.8 reduce-scatter.28
  929.5 78.4 reduce-scatter.26
where the time goes:
time: 1120 us; the launch traced here: 1110 us
  blocking collectives  572 us (51%)
  waiting for transfers between devices  346 us (31%)
  local copies, waits for them, and re-layouts  98.9 us (9%)
  matrix products  52.6 us (5%)
  other arithmetic  22.7 us (2%)
  between operations  20.4 us (2%)
    unnamed x14, waiting for transfers between devices  346 us
    psum x3, blocking collectives, local(): totals = lax.psum(jnp.stack(locals_list), ('row', 'col'))  232 us
    psum x2, blocking collectives, local(): lax.psum(jnp.stack([inner(residual, residual), inner(residual, dresidual)...  146 us
    all_gather x6, blocking collectives, apply(): lax.all_gather(stacked.astype(jnp.bfloat16), 'row', axis=0, tiled=True)  112 us
    psum x1, blocking collectives, local(): lax.psum(jnp.stack([inner(primal, primal), inner(primal, tangent)]), ('ro...  81.9 us
    unnamed x43, local copies, waits for them, and re-layouts  31.9 us
  transfers between devices with their start and end apart: 8, of which 6 were waited for; matrix products, arithmetic and copies ran while one was open for 8% of the time, Pallas kernels for 0%

commit v1 on v0

--- a/solution.py
+++ b/solution.py
@@ -11,6 +11,10 @@
 
 def inner(first, second):
     return jnp.sum(first * second)
+
+
+def total(values):
+    return lax.psum(lax.psum(values, "col"), "row")
 
 
 def taylor(hess, dhess):
@@ -59,28 +63,63 @@
 
     primal = site_tensor.astype(jnp.float32)
     tangent = site_tangent.astype(jnp.float32)
-    starting = lax.psum(jnp.stack([inner(primal, primal), inner(primal, tangent)]), ("row", "col"))
+    starting = total(jnp.stack([inner(primal, primal), inner(primal, tangent)]))
     norm_site = jnp.sqrt(starting[0])
     norm_tangent = starting[1] / norm_site
     basis = [primal / norm_site]
     tangents = [(tangent - basis[0] * norm_tangent) / norm_site]
     hess = jnp.zeros((KRYLOV, KRYLOV), jnp.float32)
     dhess = jnp.zeros((KRYLOV, KRYLOV), jnp.float32)
+    gram = jnp.zeros((KRYLOV, KRYLOV), jnp.float32)
+    cross = jnp.zeros((KRYLOV, KRYLOV), jnp.float32)
     for level in range(KRYLOV):
-        image = apply(basis[level][:, None])[:, 0]
-        dimage = apply(tangents[level][:, None])[:, 0]
+        both = apply(jnp.stack([basis[level], tangents[level]], axis=1))
+        image = both[:, 0]
+        dimage = both[:, 1]
         counted = level + 1
         locals_list = [inner(vector, image) for vector in basis]
         locals_list = locals_list + [inner(vector, image) for vector in tangents]
         locals_list = locals_list + [inner(vector, dimage) for vector in basis]
-        totals = lax.psum(jnp.stack(locals_list), ("row", "col"))
+        last = level + 1 == KRYLOV
+        if not last:
+            newest = basis[level]
+            locals_list = locals_list + [inner(image, image), inner(image, dimage)]
+            locals_list = locals_list + [inner(newest, vector) for vector in basis]
+            locals_list = locals_list + [inner(newest, vector) for vector in tangents]
+            locals_list = locals_list + [inner(vector, tangents[level]) for vector in basis[:level]]
+        totals = total(jnp.stack(locals_list))
         coeffs = totals[:counted]
         across = totals[counted : 2 * counted]
         along = totals[2 * counted : 3 * counted]
         dcoeffs = across + along
         hess = hess.at[:counted, level].set(coeffs)
         dhess = dhess.at[:counted, level].set(dcoeffs)
-        if level + 1 < KRYLOV:
+        if not last:
+            at = 3 * counted
+            squared_image = totals[at]
+            image_dimage = totals[at + 1]
+            at += 2
+            gram = gram.at[level, :counted].set(totals[at : at + counted])
+            gram = gram.at[:counted, level].set(totals[at : at + counted])
+            at += counted
+            cross = cross.at[level, :counted].set(totals[at : at + counted])
+            at += counted
+            cross = cross.at[:level, level].set(totals[at : at + level])
+            g = gram[:counted, :counted]
+            t = cross[:counted, :counted]
+            squared = (
+                squared_image
+                - 2.0 * jnp.sum(coeffs * coeffs)
+                + jnp.dot(coeffs, jnp.dot(g, coeffs, precision=lax.Precision.HIGHEST), precision=lax.Precision.HIGHEST)
+            )
+            mixed_term = (
+                image_dimage
+                - jnp.sum(dcoeffs * coeffs)
+                - jnp.sum(coeffs * across)
+                - jnp.sum(coeffs * along)
+                + jnp.dot(coeffs, jnp.dot(g, dcoeffs, precision=lax.Precision.HIGHEST), precision=lax.Precision.HIGHEST)
+                + jnp.dot(coeffs, jnp.dot(t, coeffs, precision=lax.Precision.HIGHEST), precision=lax.Precision.HIGHEST)
+            )
             residual = image
             dresidual = dimage
             for index in range(counted):
@@ -88,11 +127,6 @@
                 dresidual = (
                     dresidual - dcoeffs[index] * basis[index] - coeffs[index] * tangents[index]
                 )
-            paired = lax.psum(
-                jnp.stack([inner(residual, residual), inner(residual, dresidual)]), ("row", "col")
-            )
-            squared = paired[0]
-            mixed_term = paired[1]
             height = jnp.sqrt(squared)
             dheight = mixed_term / height
             newvec = residual / height

time: 1120 us -> 881 us (0.79)
  blocking collectives: 572 us -> 260 us
  waiting for transfers between devices: 346 us -> 389 us
  local copies, waits for them, and re-layouts: 98.9 us -> 123 us
  between operations: 20.4 us -> 34.7 us
    psum x6 -> x8, blocking collectives: 460 us -> 260 us  [total(): return lax.psum(lax.psum(values, 'col'), 'row')]
    unnamed x14 -> x11, waiting for transfers between devices: 346 us -> 225 us
    all_gather x6 -> x0, blocking collectives: 112 us -> none  [apply(): lax.all_gather(stacked.astype(jnp.bfloat16), 'row', axis=0, tiled=True)]
    all_gather x0 -> x3, waiting for transfers between devices: none -> 104 us  [apply(): lax.all_gather(stacked.astype(jnp.bfloat16), 'row', axis=0, tiled=True)]
    all_gather x1, waiting for transfers between devices: 0.02 us -> 44.7 us  [local(): left_whole = lax.all_gather(left_env, 'col', axis=1, tiled=True)]
    all_gather x1, waiting for transfers between devices: 0.02 us -> 14.8 us  [local(): right_whole = lax.all_gather(right_env, 'row', axis=0, tiled=True)]
    reshape x0 -> x3, local copies, waits for them, and re-layouts: none -> 12.9 us  [apply(): mixed.astype(jnp.bfloat16)]
    unnamed x43 -> x23, local copies, waits for them, and re-layouts: 31.9 us -> 35.7 us
  transfers between devices with their start and end apart: 8 -> 8, of which waited for: 6 -> 8; matrix products, arithmetic and copies ran while one was open for 8% -> 5% of each run, Pallas kernels for 0% -> 0%
where the time goes in v1:
time: 881 us; the launch traced here: 870 us
  waiting for transfers between devices  389 us (44%)
  blocking collectives  260 us (30%)
  local copies, waits for them, and re-layouts  123 us (14%)
  matrix products  48.2 us (5%)
  between operations  34.7 us (4%)
  other arithmetic  15.4 us (2%)
    psum x8, blocking collectives, total(): return lax.psum(lax.psum(values, 'col'), 'row')  260 us
    unnamed x11, waiting for transfers between devices  225 us
    all_gather x3, waiting for transfers between devices, apply(): lax.all_gather(stacked.astype(jnp.bfloat16), 'row', axis=0, tiled=True)  104 us
    all_gather x1, waiting for transfers between devices, local(): left_whole = lax.all_gather(left_env, 'col', axis=1, tiled=True)  44.7 us
    unnamed x23, local copies, waits for them, and re-layouts  35.7 us
    another operation x3, local copies, waits for them, and re-layouts, local(): totals = total(jnp.stack(locals_list))  18.4 us
  transfers between devices with their start and end apart: 8, of which 8 were waited for; matrix products, arithmetic and copies ran while one was open for 5% of the time, Pallas kernels for 0%

profile of v1, /device:TPU:1, one launch (start us, length us, event | category | flops | bytes accessed | tf_op | source)
XLA Modules:
  0.0 870.5 jit_solution(10881828648179970118)
XLA Ops:
  10.1 34.2 %psum.56 = f32[2]{0:T(128)S(1)} all-reduce(f32[2]{0:T(128)S(1)} %pad_maximum_fusion.3), channel_id=1, replica_groups=mesh['row'=16,'col'=16] {'col'}, use_global_device_ids=true, to_apply=%region_2.0 | all-reduce | flops 2 | bytes 16 | tf_op jit(solution)/shard_map/psum | solution.py:17
  44.3 33.8 %psum.57 = f32[2]{0:T(128)S(1)} all-reduce(f32[2]{0:T(128)S(1)} %psum.56), channel_id=1, replica_groups=mesh['row'=16,'col'=16] {'row'}, use_global_device_ids=true, to_apply=%region_3.0 | all-reduce | flops 2 | bytes 16 | tf_op jit(solution)/shard_map/psum | solution.py:17
  84.3 32.3 %all-gather.6.cloned.1.call-done = bf16[1024,2,4,64]{3,2,1,0:T(4,128)(2,1)} async-done(((bf16[64,2,4,64]{3,2,1,0:T(4,128)(2,1)}), bf16[1024,2,4,64]{3,2,1,0:T(4,128)(2,1)}) %all-gather.6.cloned.1.call-update) | async-done | bytes 1048592 | tf_op jit(solution)/shard_map/all_gather | solution.py:46
  120.7 44.7 %all-gather.8.cloned.1.call-done = bf16[64,16384]{1,0:T(8,128)(2,1)} async-done(((bf16[64,1024]{1,0:T(8,128)(2,1)}), bf16[64,16384]{1,0:T(8,128)(2,1)}) %all-gather.8.cloned.1.call-update) | async-done | bytes 2097168 | tf_op jit(solution)/shard_map/all_gather | solution.py:41
  165.5 4.8 copy.110
  178.2 4.7 reshape.536
  187.6 5.8 copy.115
  193.4 14.8 %all-gather.10.cloned.1.call-done = bf16[1024,1024]{1,0:T(8,128)(2,1)} async-done(((bf16[64,1024]{1,0:T(8,128)(2,1)}), bf16[1024,1024]{1,0:T(8,128)(2,1)}) %all-gather.10.cloned.1.call-update) | async-done | bytes 2097168 | tf_op jit(solution)/shard_map/all_gather | solution.py:42
  208.1 6.0 fusion.5
  214.1 4.8 copy.173
  218.9 5.6 reshape.685
  224.7 76.6 %reduce-scatter.10.cloned.1.call-done = f32[64,512]{1,0:T(8,128)} async-done(((f32[1024,512]{1,0:T(8,128)}), f32[64,512]{1,0:T(8,128)}) %reduce-scatter.10.cloned.1.call-update) | async-done | bytes 131088
  307.9 30.9 %psum.58 = f32[7]{0:T(128)S(1)} all-reduce(f32[7]{0:T(128)S(1)} %stack.145), channel_id=1, replica_groups=mesh['row'=16,'col'=16] {'col'}, use_global_device_ids=true, to_apply=%region_12.0 | all-reduce | flops 7 | bytes 56 | tf_op jit(solution)/shard_map/psum | solution.py:17
  338.8 32.9 %psum.59 = f32[7]{0:T(128)S(1)} all-reduce(f32[7]{0:T(128)S(1)} %psum.58), channel_id=1, replica_groups=mesh['row'=16,'col'=16] {'row'}, use_global_device_ids=true, to_apply=%region_13.0 | all-reduce | flops 7 | bytes 56 | tf_op jit(solution)/shard_map/psum | solution.py:17
  385.0 35.9 %all-gather.12.cloned.1.call-done = bf16[1024,2,4,64]{3,2,1,0:T(4,128)(2,1)} async-done(((bf16[64,2,4,64]{3,2,1,0:T(4,128)(2,1)}), bf16[1024,2,4,64]{3,2,1,0:T(4,128)(2,1)}) %all-gather.12.cloned.1.call-update) | async-done | bytes 1048592 | tf_op jit(solution)/shard_map/all_gather | solution.py:46
  428.4 4.7 reshape.543
  433.1 4.7 fusion.12
  437.8 5.8 copy.123
  443.6 6.0 fusion.3
  449.6 4.8 copy.175
  454.3 5.6 reshape.687
  462.5 74.2 %reduce-scatter.12.cloned.1.call-done = f32[64,512]{1,0:T(8,128)} async-done(((f32[1024,512]{1,0:T(8,128)}), f32[64,512]{1,0:T(8,128)}) %reduce-scatter.12.cloned.1.call-update) | async-done | bytes 131088
  538.9 8.2 stack.162
  547.7 30.9 %psum.60 = f32[13]{0:T(128)S(1)} all-reduce(f32[13]{0:T(128)S(1)} %stack.162), channel_id=1, replica_groups=mesh['row'=16,'col'=16] {'col'}, use_global_device_ids=true, to_apply=%region_28.0 | all-reduce | flops 13 | bytes 104 | tf_op jit(solution)/shard_map/psum | solution.py:17
  578.6 33.1 %psum.61 = f32[13]{0:T(128)S(1)} all-reduce(f32[13]{0:T(128)S(1)} %psum.60), channel_id=1, replica_groups=mesh['row'=16,'col'=16] {'row'}, use_global_device_ids=true, to_apply=%region_29.0 | all-reduce | flops 13 | bytes 104 | tf_op jit(solution)/shard_map/psum | solution.py:17
  631.8 35.9 %all-gather.14.cloned.1.call-done = bf16[1024,2,4,64]{3,2,1,0:T(4,128)(2,1)} async-done(((bf16[64,2,4,64]{3,2,1,0:T(4,128)(2,1)}), bf16[1024,2,4,64]{3,2,1,0:T(4,128)(2,1)}) %all-gather.14.cloned.1.call-update) | async-done | bytes 1048592 | tf_op jit(solution)/shard_map/all_gather | solution.py:46
  681.9 5.8 copy.132
  695.5 5.6 reshape.689
  705.0 72.9 %reduce-scatter.14.cloned.1.call-done = f32[64,512]{1,0:T(8,128)} async-done(((f32[1024,512]{1,0:T(8,128)}), f32[64,512]{1,0:T(8,128)}) %reduce-scatter.14.cloned.1.call-update) | async-done | bytes 131088
  780.1 5.7 stack.175
  785.9 30.9 %psum.62 = f32[9]{0:T(128)S(1)} all-reduce(f32[9]{0:T(128)S(1)} %stack.175), channel_id=1, replica_groups=mesh['row'=16,'col'=16] {'col'}, use_global_device_ids=true, to_apply=%region_45.0 | all-reduce | flops 9 | bytes 72 | tf_op jit(solution)/shard_map/psum | solution.py:17
  816.9 32.9 %psum.63 = f32[9]{0:T(128)S(1)} all-reduce(f32[9]{0:T(128)S(1)} %psum.62), channel_id=1, replica_groups=mesh['row'=16,'col'=16] {'row'}, use_global_device_ids=true, to_apply=%region_46.0 | all-reduce | flops 9 | bytes 72 | tf_op jit(solution)/shard_map/psum | solution.py:17
  (146 shorter events, 100.6 us)
Async XLA Ops:
  7.2 109.4 %all-gather.6.cloned.1.call-start = ((), (), s32[]{:S(2)}) async-start(), calls=%async_computation.3 | async-start | bytes 2228224 | tf_op jit(solution)/shard_map/all_gather | solution.py:46
  81.8 83.7 %all-gather.8.cloned.1.call-start = ((), (), s32[]{:S(2)}) async-start(), calls=%async_computation.4 | async-start | bytes 2228224 | tf_op jit(solution)/shard_map/all_gather | solution.py:41
  82.5 125.6 %all-gather.10.cloned.1.call-start = ((), (), s32[]{:S(2)}) async-start(), calls=%async_computation.5 | async-start | bytes 2228224 | tf_op jit(solution)/shard_map/all_gather | solution.py:42
  83.3 218.0 %reduce-scatter.10.cloned.1.call-start = ((), (), s32[]{:S(2)}) async-start(), calls=%async_computation.8 | async-start | bytes 2228224
  224.5 78.0 %copy-start.2 = (f32[4]{0:T(128)S(1)}, f32[4]{0:T(128)}, u32[]{:S(2)}) copy-start(f32[4]{0:T(128)} %param.47) | copy-start | bytes 52
  224.5 78.1 %copy-start = (bf16[64,4,64]{2,1,0:T(4,128)(2,1)S(1)}, bf16[64,4,64]{2,1,0:T(4,128)(2,1)}, u32[]{:S(2)}) copy-start(bf16[64,4,64]{2,1,0:T(4,128)(2,1)} %param.42) | copy-start | bytes 98308
  224.5 78.1 %copy-start.1 = (bf16[64,4,64]{2,1,0:T(4,128)(2,1)S(1)}, bf16[64,4,64]{2,1,0:T(4,128)(2,1)}, u32[]{:S(2)}) copy-start(bf16[64,4,64]{2,1,0:T(4,128)(2,1)} %param.43) | copy-start | bytes 98308
  224.5 196.3 %all-gather.12.cloned.1.call-start = ((), (), s32[]{:S(2)}) async-start(), calls=%async_computation.6 | async-start | bytes 2228224 | tf_op jit(solution)/shard_map/all_gather | solution.py:46
  384.9 151.7 %reduce-scatter.12.cloned.1.call-start = ((), (), s32[]{:S(2)}) async-start(), calls=%async_computation.9 | async-start | bytes 2228224
  460.0 207.7 %all-gather.14.cloned.1.call-start = ((), (), s32[]{:S(2)}) async-start(), calls=%async_computation.7 | async-start | bytes 2228224 | tf_op jit(solution)/shard_map/all_gather | solution.py:46
  631.8 146.2 %reduce-scatter.14.cloned.1.call-start = ((), (), s32[]{:S(2)}) async-start(), calls=%async_computation.10 | async-start | bytes 2228224
  701.1 148.9 %copy-start.3 = (f32[3,1]{0,1:T(1,128)S(1)}, f32[3,1]{0,1:T(1,128)}, u32[]{:S(2)}) copy-start(f32[3,1]{0,1:T(1,128)} %constant.468) | copy-start | bytes 40
Sparse Core Ops, SparseCore 0:
  81.9 34.6 all-gather.5
  119.1 46.3 all-gather.7
  167.3 40.7 all-gather.9
  224.6 76.6 reduce-scatter.9
  385.1 35.7 all-gather.11
  460.1 76.5 reduce-scatter.11
  631.9 35.7 all-gather.13
  701.3 76.5 reduce-scatter.13

commit v2 on v1

--- a/solution.py
+++ b/solution.py
@@ -58,7 +58,11 @@
             channel, right_whole, (((1,), (1,)), ((), ())), preferred_element_type=jnp.float32
         )
         partial_rows = partial_rows.reshape(rows_here, panels, physical, partial_rows.shape[1])
-        summed = lax.psum_scatter(partial_rows, "col", scatter_dimension=3, tiled=True)
+        blocks = lax.psum(1, "col")
+        split = partial_rows.reshape(
+            rows_here, panels, physical, blocks, partial_rows.shape[3] // blocks
+        )
+        summed = jnp.sum(lax.all_to_all(split, "col", 3, 3, tiled=False), axis=3)
         return summed - dissipation[None, None, :, None] * stacked
 
     primal = site_tensor.astype(jnp.float32)

time: 881 us -> 768 us (0.87)
  waiting for transfers between devices: 389 us -> 216 us
  other arithmetic: 15.4 us -> 45.2 us
  blocking collectives: 260 us -> 287 us
  local copies, waits for them, and re-layouts: 123 us -> 109 us
  starting transfers between devices: 0.5 us -> 13.5 us
    unnamed x11 -> x5, waiting for transfers between devices: 225 us -> 1.43 us
    all_to_all x0 -> x2, waiting for transfers between devices: none -> 52 us  [apply(): summed = jnp.sum(lax.all_to_all(split, 'col', 3, 3, tiled=False), axis=3)]
    all_to_all x0 -> x1, blocking collectives: none -> 33.9 us  [apply(): summed = jnp.sum(lax.all_to_all(split, 'col', 3, 3, tiled=False), axis=3)]
    all_to_all x0 -> x3, other arithmetic: none -> 21.6 us  [apply(): summed = jnp.sum(lax.all_to_all(split, 'col', 3, 3, tiled=False), axis=3)]
    all_to_all x0 -> x2, starting transfers between devices: none -> 13.2 us  [apply(): summed = jnp.sum(lax.all_to_all(split, 'col', 3, 3, tiled=False), axis=3)]
    unnamed x23 -> x27, local copies, waits for them, and re-layouts: 35.7 us -> 27 us
  transfers between devices with their start and end apart: 8 -> 7, of which waited for: 8 -> 7; matrix products, arithmetic and copies ran while one was open for 5% -> 5% of each run, Pallas kernels for 0% -> 0%
where the time goes in v2:
time: 768 us; the launch traced here: 758 us
  blocking collectives  287 us (37%)
  waiting for transfers between devices  216 us (28%)
  local copies, waits for them, and re-layouts  109 us (14%)
  matrix products  51 us (7%)
  other arithmetic  45.2 us (6%)
  between operations  35.9 us (5%)
  starting transfers between devices  13.5 us (2%)
    psum x8, blocking collectives, total(): return lax.psum(lax.psum(values, 'col'), 'row')  253 us
    all_gather x3, waiting for transfers between devices, apply(): lax.all_gather(stacked.astype(jnp.bfloat16), 'row', axis=0, tiled=True)  100 us
    all_to_all x2, waiting for transfers between devices, apply(): summed = jnp.sum(lax.all_to_all(split, 'col', 3, 3, tiled=False), axis=3)  52 us
    all_gather x1, waiting for transfers between devices, local(): left_whole = lax.all_gather(left_env, 'col', axis=1, tiled=True)  45.9 us
    all_to_all x1, blocking collectives, apply(): summed = jnp.sum(lax.all_to_all(split, 'col', 3, 3, tiled=False), axis=3)  33.9 us
    unnamed x27, local copies, waits for them, and re-layouts  27 us
    dot_general x3, matrix products, apply(): lax.dot_general(channel, right_whole, (((1,), (1,)), ((), ())), preferred...  23.2 us
    all_to_all x3, other arithmetic, apply(): summed = jnp.sum(lax.all_to_all(split, 'col', 3, 3, tiled=False), axis=3)  21.6 us
  transfers between devices with their start and end apart: 7, of which 7 were waited for; matrix products, arithmetic and copies ran while one was open for 5% of the time, Pallas kernels for 0%

profile of v2, /device:TPU:1, one launch (start us, length us, event | category | flops | bytes accessed | tf_op | source)
XLA Modules:
  0.0 758.4 jit_solution(17922778366291939075)
XLA Ops:
  10.1 34.2 %psum.56 = f32[2]{0:T(128)S(1)} all-reduce(f32[2]{0:T(128)S(1)} %pad_maximum_fusion.3), channel_id=1, replica_groups=mesh['row'=16,'col'=16] {'col'}, use_global_device_ids=true, to_apply=%region_2.0 | all-reduce | flops 2 | bytes 16 | tf_op jit(solution)/shard_map/psum | solution.py:17
  44.3 33.8 %psum.57 = f32[2]{0:T(128)S(1)} all-reduce(f32[2]{0:T(128)S(1)} %psum.56), channel_id=1, replica_groups=mesh['row'=16,'col'=16] {'row'}, use_global_device_ids=true, to_apply=%region_3.0 | all-reduce | flops 2 | bytes 16 | tf_op jit(solution)/shard_map/psum | solution.py:17
  84.3 32.3 %all-gather.6.cloned.1.call-done = bf16[1024,2,4,64]{3,2,1,0:T(4,128)(2,1)} async-done(((bf16[64,2,4,64]{3,2,1,0:T(4,128)(2,1)}), bf16[1024,2,4,64]{3,2,1,0:T(4,128)(2,1)}) %all-gather.6.cloned.1.call-update) | async-done | bytes 1048592 | tf_op jit(solution)/shard_map/all_gather | solution.py:46
  119.5 45.9 %all-gather.8.cloned.1.call-done = bf16[64,16384]{1,0:T(8,128)(2,1)} async-done(((bf16[64,1024]{1,0:T(8,128)(2,1)}), bf16[64,16384]{1,0:T(8,128)(2,1)}) %all-gather.8.cloned.1.call-update) | async-done | bytes 2097168 | tf_op jit(solution)/shard_map/all_gather | solution.py:41
  165.5 4.8 copy.46
  186.4 4.9 copy.51
  191.3 16.8 %all-gather.10.cloned.1.call-done = bf16[1024,1024]{1,0:T(8,128)(2,1)} async-done(((bf16[64,1024]{1,0:T(8,128)(2,1)}), bf16[1024,1024]{1,0:T(8,128)(2,1)}) %all-gather.10.cloned.1.call-update) | async-done | bytes 2097168 | tf_op jit(solution)/shard_map/all_gather | solution.py:42
  208.1 7.7 %convolution_bitcast_fusion.52 = f32[16,2,4,64,64]{4,3,2,1,0:T(8,128)} fusion(bf16[64,2,4,1024,1]{0,3,2,1,4:T(8,128)(2,1)S(1)} %bitcast.661, bf16[16,64,1024,1,1]{2,1,4,3,0:T(8,128)(2,1)} %bitcast.669), kind=kOutput, calls=%fused_computation.260 | convolution fusion | flops 1073741824 | bytes 5242880 | tf_op jit(solution)/shard_map/dot_general | solution.py:57
  220.4 33.9 %all_to_all.15 = f32[16,1,32768]{2,1,0:T(1,128)} all-to-all(f32[16,1,32768]{2,1,0:T(1,128)S(1)} %reshape.688), channel_id=1, replica_groups=mesh['row'=16,'col'=16] {'col'}, dimensions={0} | all-to-all | bytes 4194304 | tf_op jit(solution)/shard_map/all_to_all | solution.py:65
  254.8 7.2 reduce.48
  273.0 31.2 %psum.58 = f32[7]{0:T(128)S(1)} all-reduce(f32[7]{0:T(128)S(1)} %stack.145), channel_id=1, replica_groups=mesh['row'=16,'col'=16] {'col'}, use_global_device_ids=true, to_apply=%region_12.0 | all-reduce | flops 7 | bytes 56 | tf_op jit(solution)/shard_map/psum | solution.py:17
  304.2 31.0 %psum.59 = f32[7]{0:T(128)S(1)} all-reduce(f32[7]{0:T(128)S(1)} %psum.58), channel_id=1, replica_groups=mesh['row'=16,'col'=16] {'row'}, use_global_device_ids=true, to_apply=%region_13.0 | all-reduce | flops 7 | bytes 56 | tf_op jit(solution)/shard_map/psum | solution.py:17
  349.9 33.7 %all-gather.12.cloned.1.call-done = bf16[1024,2,4,64]{3,2,1,0:T(4,128)(2,1)} async-done(((bf16[64,2,4,64]{3,2,1,0:T(4,128)(2,1)}), bf16[1024,2,4,64]{3,2,1,0:T(4,128)(2,1)}) %all-gather.12.cloned.1.call-update) | async-done | bytes 1048592 | tf_op jit(solution)/shard_map/all_gather | solution.py:46
  395.5 4.9 copy.61
  400.4 7.8 %convolution_bitcast_fusion.51 = f32[16,2,4,64,64]{4,3,2,1,0:T(8,128)} fusion(bf16[64,2,4,1024,1]{0,3,2,1,4:T(8,128)(2,1)S(1)} %bitcast.663, bf16[16,64,1024,1,1]{2,1,4,3,0:T(8,128)(2,1)} %bitcast.670), kind=kOutput, calls=%fused_computation.259 | convolution fusion | flops 1073741824 | bytes 5242880 | tf_op jit(solution)/shard_map/dot_general | solution.py:57
  408.2 5.5 reshape.690
  413.7 6.6 all-to-all-start.1
  423.0 26.6 %all-to-all-done.1 = f32[16,1,32768]{2,1,0:T(1,128)} async-done(((f32[16,1,32768]{2,1,0:T(1,128)}), f32[16,1,32768]{2,1,0:T(1,128)}, u32[]{:S(2)}, u32[]{:S(2)}) %all-to-all-start.1) | async-done | bytes 2097184 | tf_op jit(solution)/shard_map/all_to_all | solution.py:65
  449.5 7.2 reduce.49
  463.4 8.2 %stack.162 = f32[13]{0:T(128)S(1)} concatenate(f32[1]{0:T(128)} %bitcast.52, f32[1]{0:T(128)} %bitcast.53, f32[1]{0:T(128)} %bitcast.54, f32[1]{0:T(128)} %bitcast.55, f32[1]{0:T(128)} %bitcast.57, f32[1]{0:T(128)} %bitcast.58, f32[1]{0:T(128)} %bitcast.59, f32[1]{0:T(128)} %bitcast.60, f32[1]{0:T(128)} %bitcast.61, f32[1]{0:T(128)} %bitcast.62, f32[1]{0:T(128)} %bitcast.63, ...), dimensions={0} | concatenate | bytes 104 | tf_op jit(solution)/shard_map/stack | solution.py:94
  472.4 29.0 %psum.60 = f32[13]{0:T(128)S(1)} all-reduce(f32[13]{0:T(128)S(1)} %stack.162), channel_id=1, replica_groups=mesh['row'=16,'col'=16] {'col'}, use_global_device_ids=true, to_apply=%region_28.0 | all-reduce | flops 13 | bytes 104 | tf_op jit(solution)/shard_map/psum | solution.py:17
  501.4 32.5 %psum.61 = f32[13]{0:T(128)S(1)} all-reduce(f32[13]{0:T(128)S(1)} %psum.60), channel_id=1, replica_groups=mesh['row'=16,'col'=16] {'row'}, use_global_device_ids=true, to_apply=%region_29.0 | all-reduce | flops 13 | bytes 104 | tf_op jit(solution)/shard_map/psum | solution.py:17
  554.3 34.1 %all-gather.14.cloned.1.call-done = bf16[1024,2,4,64]{3,2,1,0:T(4,128)(2,1)} async-done(((bf16[64,2,4,64]{3,2,1,0:T(4,128)(2,1)}), bf16[1024,2,4,64]{3,2,1,0:T(4,128)(2,1)}) %all-gather.14.cloned.1.call-update) | async-done | bytes 1048592 | tf_op jit(solution)/shard_map/all_gather | solution.py:46
  602.7 4.9 copy.72
  607.6 7.8 %convolution_bitcast_fusion.50 = f32[16,2,4,64,64]{4,3,2,1,0:T(8,128)} fusion(bf16[64,2,4,1024,1]{0,3,2,1,4:T(8,128)(2,1)S(1)} %bitcast.662, bf16[16,64,1024,1,1]{2,1,4,3,0:T(8,128)(2,1)} %bitcast.671), kind=kOutput, calls=%fused_computation.258 | convolution fusion | flops 1073741824 | bytes 5242880 | tf_op jit(solution)/shard_map/dot_general | solution.py:57
  615.4 5.5 reshape.692
  620.9 6.6 all-to-all-start.2
  631.3 25.4 %all-to-all-done.2 = f32[16,1,32768]{2,1,0:T(1,128)} async-done(((f32[16,1,32768]{2,1,0:T(1,128)}), f32[16,1,32768]{2,1,0:T(1,128)}, u32[]{:S(2)}, u32[]{:S(2)}) %all-to-all-start.2) | async-done | bytes 2097184 | tf_op jit(solution)/shard_map/all_to_all | solution.py:65
  656.8 7.2 reduce.50
  670.6 5.7 stack.175
  676.4 29.0 %psum.62 = f32[9]{0:T(128)S(1)} all-reduce(f32[9]{0:T(128)S(1)} %stack.175), channel_id=1, replica_groups=mesh['row'=16,'col'=16] {'col'}, use_global_device_ids=true, to_apply=%region_45.0 | all-reduce | flops 9 | bytes 72 | tf_op jit(solution)/shard_map/psum | solution.py:17
  705.5 32.5 %psum.63 = f32[9]{0:T(128)S(1)} all-reduce(f32[9]{0:T(128)S(1)} %psum.62), channel_id=1, replica_groups=mesh['row'=16,'col'=16] {'row'}, use_global_device_ids=true, to_apply=%region_46.0 | all-reduce | flops 9 | bytes 72 | tf_op jit(solution)/shard_map/psum | solution.py:17
  (153 shorter events, 118.1 us)
Async XLA Ops:
  7.2 109.4 %all-gather.6.cloned.1.call-start = ((), (), s32[]{:S(2)}) async-start(), calls=%async_computation.3 | async-start | bytes 2228224 | tf_op jit(solution)/shard_map/all_gather | solution.py:46
  81.8 83.7 %all-gather.8.cloned.1.call-start = ((), (), s32[]{:S(2)}) async-start(), calls=%async_computation.4 | async-start | bytes 2228224 | tf_op jit(solution)/shard_map/all_gather | solution.py:41
  82.5 125.6 %all-gather.10.cloned.1.call-start = ((), (), s32[]{:S(2)}) async-start(), calls=%async_computation.5 | async-start | bytes 2228224 | tf_op jit(solution)/shard_map/all_gather | solution.py:42
  83.3 300.3 %all-gather.12.cloned.1.call-start = ((), (), s32[]{:S(2)}) async-start(), calls=%async_computation.6 | async-start | bytes 2228224 | tf_op jit(solution)/shard_map/all_gather | solution.py:46
  84.3 97.4 %copy-start.5 = (bf16[16,16,4,4,1,1]{0,1,2,3,5,4:T(8,128)(2,1)}, bf16[16,16,4,4,1,1]{0,1,2,3,5,4:T(8,128)(2,1)S(1)}, u32[]{:S(2)}) copy-start(bf16[16,16,4,4,1,1]{0,1,2,3,5,4:T(8,128)(2,1)S(1)} %copy.80) | copy-start | bytes 24580
  174.7 2.3 copy-start.2
  265.0 2.7 copy-start.7
  265.0 2.8 copy-start
  265.0 2.8 copy-start.1
  349.1 37.4 %copy-start.3 = (bf16[64,1024,16]{1,0,2:T(8,128)(2,1)S(1)}, bf16[64,1024,16]{1,0,2:T(8,128)(2,1)}, u32[]{:S(2)}) copy-start(bf16[64,1024,16]{1,0,2:T(8,128)(2,1)} %copy-done.2) | copy-start | bytes 6291460
  388.8 3.6 copy-start.6
  413.7 35.9 %all-to-all-start.1 = ((f32[16,1,32768]{2,1,0:T(1,128)}), f32[16,1,32768]{2,1,0:T(1,128)}, u32[]{:S(2)}, u32[]{:S(2)}) async-start(f32[16,1,32768]{2,1,0:T(1,128)} %reshape.690), calls=%async_computation.1 | async-start | bytes 4194304 | tf_op jit(solution)/shard_map/all_to_all | solution.py:65
  420.2 168.2 %all-gather.14.cloned.1.call-start = ((), (), s32[]{:S(2)}) async-start(), calls=%async_computation.7 | async-start | bytes 2228224 | tf_op jit(solution)/shard_map/all_gather | solution.py:46
  553.5 39.0 %copy-start.4 = (bf16[64,1024,16]{1,0,2:T(8,128)(2,1)S(1)}, bf16[64,1024,16]{1,0,2:T(8,128)(2,1)}, u32[]{:S(2)}) copy-start(bf16[64,1024,16]{1,0,2:T(8,128)(2,1)} %copy-done.2) | copy-start | bytes 6291460
  620.9 35.9 %all-to-all-start.2 = ((f32[16,1,32768]{2,1,0:T(1,128)}), f32[16,1,32768]{2,1,0:T(1,128)}, u32[]{:S(2)}, u32[]{:S(2)}) async-start(f32[16,1,32768]{2,1,0:T(1,128)} %reshape.692), calls=%async_computation.2 | async-start | bytes 4194304 | tf_op jit(solution)/shard_map/all_to_all | solution.py:65
  667.0 71.3 %copy-start.8 = (f32[3,1]{0,1:T(1,128)S(1)}, f32[3,1]{0,1:T(1,128)}, u32[]{:S(2)}) copy-start(f32[3,1]{0,1:T(1,128)} %constant.468) | copy-start | bytes 40
Sparse Core Ops, SparseCore 0:
  81.9 34.6 all-gather.5
  119.1 46.3 all-gather.7
  167.3 40.7 all-gather.9
  350.0 33.5 all-gather.11
  554.5 33.9 all-gather.13

commit v3 on v2

--- a/solution.py
+++ b/solution.py
@@ -41,9 +41,9 @@
     left_whole = lax.all_gather(left_env, "col", axis=1, tiled=True)
     right_whole = lax.all_gather(right_env, "row", axis=0, tiled=True)
 
-    def apply(stacked):
+    def apply(stacked, whole_stacked):
         panels = stacked.shape[1]
-        whole = lax.all_gather(stacked.astype(jnp.bfloat16), "row", axis=0, tiled=True)
+        whole = whole_stacked.astype(jnp.bfloat16)
         flat = whole.reshape(whole.shape[0], panels * physical * cols_here)
         left_three = left_whole.reshape(rows_here, flat.shape[0], channels)
         mixed = lax.dot_general(
@@ -72,14 +72,28 @@
     norm_tangent = starting[1] / norm_site
     basis = [primal / norm_site]
     tangents = [(tangent - basis[0] * norm_tangent) / norm_site]
+    inputs_whole = lax.all_gather(
+        jnp.stack([site_tensor, site_tangent], axis=1), "row", axis=0, tiled=True
+    ).astype(jnp.float32)
+    primal_whole = inputs_whole[:, 0]
+    tangent_whole = inputs_whole[:, 1]
+    basis_whole = [primal_whole / norm_site]
+    tangents_whole = [(tangent_whole - basis_whole[0] * norm_tangent) / norm_site]
     hess = jnp.zeros((KRYLOV, KRYLOV), jnp.float32)
     dhess = jnp.zeros((KRYLOV, KRYLOV), jnp.float32)
     gram = jnp.zeros((KRYLOV, KRYLOV), jnp.float32)
     cross = jnp.zeros((KRYLOV, KRYLOV), jnp.float32)
     for level in range(KRYLOV):
-        both = apply(jnp.stack([basis[level], tangents[level]], axis=1))
+        both = apply(
+            jnp.stack([basis[level], tangents[level]], axis=1),
+            jnp.stack([basis_whole[level], tangents_whole[level]], axis=1),
+        )
         image = both[:, 0]
         dimage = both[:, 1]
+        if level + 1 < KRYLOV:
+            both_whole = lax.all_gather(both, "row", axis=0, tiled=True)
+            image_whole = both_whole[:, 0]
+            dimage_whole = both_whole[:, 1]
         counted = level + 1
         locals_list = [inner(vector, image) for vector in basis]
         locals_list = locals_list + [inner(vector, image) for vector in tangents]
@@ -136,6 +150,18 @@
             newvec = residual / height
             basis.append(newvec)
             tangents.append((dresidual - newvec * dheight) / height)
+            residual_whole = image_whole
+            dresidual_whole = dimage_whole
+            for index in range(counted):
+                residual_whole = residual_whole - coeffs[index] * basis_whole[index]
+                dresidual_whole = (
+                    dresidual_whole
+                    - dcoeffs[index] * basis_whole[index]
+                    - coeffs[index] * tangents_whole[index]
+                )
+            newvec_whole = residual_whole / height
+            basis_whole.append(newvec_whole)
+            tangents_whole.append((dresidual_whole - newvec_whole * dheight) / height)
             hess = hess.at[level + 1, level].set(height)
             dhess = dhess.at[level + 1, level].set(dheight)
     coeff, dcoeff = taylor(hess, dhess)

time: 768 us -> 675 us (0.88)
  waiting for transfers between devices: 216 us -> 111 us
  blocking collectives: 287 us -> 253 us
  local copies, waits for them, and re-layouts: 109 us -> 132 us
  other arithmetic: 45.2 us -> 61.2 us
    all_gather x3, waiting for transfers between devices: 100 us -> 0.04 us  [the longest x2 0.02 us: local(): both_whole = lax.all_gather(both, 'row', axis=0, tiled=True)]
    all_to_all x1 -> x0, blocking collectives: 33.9 us -> none  [apply(): summed = jnp.sum(lax.all_to_all(split, 'col', 3, 3, tiled=False), axis=3)]
    all_gather x1, waiting for transfers between devices: 45.9 us -> 14.1 us  [local(): left_whole = lax.all_gather(left_env, 'col', axis=1, tiled=True)]
    all_to_all x2 -> x3, waiting for transfers between devices: 52 us -> 79 us  [apply(): summed = jnp.sum(lax.all_to_all(split, 'col', 3, 3, tiled=False), axis=3)]
    unnamed x27 -> x37, local copies, waits for them, and re-layouts: 27 us -> 44.6 us
    another operation x4 -> x11, other arithmetic: 2.37 us -> 13.7 us
    slice x2 -> x4, local copies, waits for them, and re-layouts: 1.31 us -> 10.3 us  [the longest x2 9.06 us: local(): image_whole = both_whole[:, 0]]
    all_to_all x2 -> x3, starting transfers between devices: 13.2 us -> 15.7 us  [apply(): summed = jnp.sum(lax.all_to_all(split, 'col', 3, 3, tiled=False), axis=3)]
  transfers between devices with their start and end apart: 7 -> 8, of which waited for: 7 -> 5; matrix products, arithmetic and copies ran while one was open for 5% -> 12% of each run, Pallas kernels for 0% -> 0%
where the time goes in v3:
time: 675 us; the launch traced here: 665 us
  blocking collectives  253 us (37%)
  local copies, waits for them, and re-layouts  132 us (20%)
  waiting for transfers between devices  111 us (16%)
  other arithmetic  61.2 us (9%)
  matrix products  55.4 us (8%)
  between operations  35.3 us (5%)
  starting transfers between devices  16.3 us (2%)
    psum x8, blocking collectives, total(): return lax.psum(lax.psum(values, 'col'), 'row')  253 us
    all_to_all x3, waiting for transfers between devices, apply(): summed = jnp.sum(lax.all_to_all(split, 'col', 3, 3, tiled=False), axis=3)  79 us
    unnamed x37, local copies, waits for them, and re-layouts  44.6 us
    dot_general x3, matrix products, apply(): lax.dot_general(channel, right_whole, (((1,), (1,)), ((), ())), preferred...  25.2 us
    all_to_all x3, other arithmetic, apply(): summed = jnp.sum(lax.all_to_all(split, 'col', 3, 3, tiled=False), axis=3)  24.4 us
    another operation x3, local copies, waits for them, and re-layouts, local(): totals = total(jnp.stack(locals_list))  18.2 us
    all_gather x1, waiting for transfers between devices, local(): right_whole = lax.all_gather(right_env, 'row', axis=0, tiled=True)  16.6 us
    convert_element_type x3, local copies, waits for them, and re-layouts, apply(): channel.astype(jnp.bfloat16)  16.5 us
  transfers between devices with their start and end apart: 8, of which 5 were waited for; matrix products, arithmetic and copies ran while one was open for 12% of the time, Pallas kernels for 0%

profile of v3, /device:TPU:1, one launch (start us, length us, event | category | flops | bytes accessed | tf_op | source)
XLA Modules:
  0.0 664.5 jit_solution(18109906515417911754)
XLA Ops:
  13.2 34.2 %psum.56 = f32[2]{0:T(128)S(1)} all-reduce(f32[2]{0:T(128)S(1)} %pad_maximum_fusion.4), channel_id=1, replica_groups=mesh['row'=16,'col'=16] {'col'}, use_global_device_ids=true, to_apply=%region_2.0 | all-reduce | flops 2 | bytes 16 | tf_op jit(solution)/shard_map/psum | solution.py:17
  47.4 33.8 %psum.57 = f32[2]{0:T(128)S(1)} all-reduce(f32[2]{0:T(128)S(1)} %psum.56), channel_id=1, replica_groups=mesh['row'=16,'col'=16] {'row'}, use_global_device_ids=true, to_apply=%region_3.0 | all-reduce | flops 2 | bytes 16 | tf_op jit(solution)/shard_map/psum | solution.py:17
  88.8 14.1 %all-gather.8.cloned.1.call-done = bf16[64,16384]{1,0:T(8,128)(2,1)} async-done(((bf16[64,1024]{1,0:T(8,128)(2,1)}), bf16[64,16384]{1,0:T(8,128)(2,1)}) %all-gather.8.cloned.1.call-update) | async-done | bytes 2097168 | tf_op jit(solution)/shard_map/all_gather | solution.py:41
  102.9 4.8 copy.47
  107.7 5.5 copy.49
  118.5 4.7 fusion.3
  123.2 5.8 copy.52
  129.0 16.6 %all-gather.10.cloned.1.call-done = bf16[1024,1024]{1,0:T(8,128)(2,1)} async-done(((bf16[64,1024]{1,0:T(8,128)(2,1)}), bf16[1024,1024]{1,0:T(8,128)(2,1)}) %all-gather.10.cloned.1.call-update) | async-done | bytes 2097168 | tf_op jit(solution)/shard_map/all_gather | solution.py:42
  145.6 8.7 %convolution_bitcast_fusion.52 = f32[16,2,4,64,64]{4,3,2,1,0:T(8,128)} fusion(bf16[64,2,4,1024,1]{0,3,2,1,4:T(8,128)(2,1)} %bitcast.659, bf16[16,64,1024,1,1]{2,1,4,3,0:T(8,128)(2,1)} %bitcast.669), kind=kOutput, calls=%fused_computation.275 | convolution fusion | flops 1073741824 | bytes 5242880 | tf_op jit(solution)/shard_map/dot_general | solution.py:57
  154.3 5.5 reshape.703
  159.8 6.7 %all-to-all-start = ((f32[16,1,32768]{2,1,0:T(1,128)}), f32[16,1,32768]{2,1,0:T(1,128)}, u32[]{:S(2)}, u32[]{:S(2)}) async-start(f32[16,1,32768]{2,1,0:T(1,128)} %reshape.703), calls=%async_computation | async-start | bytes 4194304 | tf_op jit(solution)/shard_map/all_to_all | solution.py:65
  166.8 29.0 %all-to-all-done = f32[16,1,32768]{2,1,0:T(1,128)} async-done(((f32[16,1,32768]{2,1,0:T(1,128)}), f32[16,1,32768]{2,1,0:T(1,128)}, u32[]{:S(2)}, u32[]{:S(2)}) %all-to-all-start) | async-done | bytes 2097184 | tf_op jit(solution)/shard_map/all_to_all | solution.py:65
  196.2 8.6 %reduce.48 = f32[16,32768]{1,0:T(8,128)} reduce(f32[16,1,32768]{2,1,0:T(1,128)} %all-to-all-done, f32[]{:T(128)} %broadcast.401), dimensions={1}, to_apply=%all_to_all.9.reduce_sub_computation | reduce | bytes 4194308 | tf_op jit(solution)/shard_map/all_to_all | solution.py:65
  217.9 29.0 %psum.58 = f32[7]{0:T(128)S(1)} all-reduce(f32[7]{0:T(128)S(1)} %stack.176), channel_id=1, replica_groups=mesh['row'=16,'col'=16] {'col'}, use_global_device_ids=true, to_apply=%region_12.0 | all-reduce | flops 7 | bytes 56 | tf_op jit(solution)/shard_map/psum | solution.py:17
  246.9 32.9 %psum.59 = f32[7]{0:T(128)S(1)} all-reduce(f32[7]{0:T(128)S(1)} %psum.58), channel_id=1, replica_groups=mesh['row'=16,'col'=16] {'row'}, use_global_device_ids=true, to_apply=%region_13.0 | all-reduce | flops 7 | bytes 56 | tf_op jit(solution)/shard_map/psum | solution.py:17
  317.1 5.8 copy.63
  322.9 8.7 %convolution_bitcast_fusion.51 = f32[16,2,4,64,64]{4,3,2,1,0:T(8,128)} fusion(bf16[64,2,4,1024,1]{0,3,2,1,4:T(8,128)(2,1)} %bitcast.661, bf16[16,64,1024,1,1]{2,1,4,3,0:T(8,128)(2,1)} %bitcast.670), kind=kOutput, calls=%fused_computation.274 | convolution fusion | flops 1073741824 | bytes 5242880 | tf_op jit(solution)/shard_map/dot_general | solution.py:57
  331.6 5.5 reshape.705
  343.4 27.4 %all-to-all-done.1 = f32[16,1,32768]{2,1,0:T(1,128)} async-done(((f32[16,1,32768]{2,1,0:T(1,128)}), f32[16,1,32768]{2,1,0:T(1,128)}, u32[]{:S(2)}, u32[]{:S(2)}) %all-to-all-start.1) | async-done | bytes 2097184 | tf_op jit(solution)/shard_map/all_to_all | solution.py:65
  370.8 8.6 %reduce.49 = f32[16,32768]{1,0:T(8,128)} reduce(f32[16,1,32768]{2,1,0:T(1,128)} %all-to-all-done.1, f32[]{:T(128)} %broadcast.401), dimensions={1}, to_apply=%all_to_all.10.reduce_sub_computation | reduce | bytes 4194308 | tf_op jit(solution)/shard_map/all_to_all | solution.py:65
  392.4 8.1 %stack.194 = f32[13]{0:T(128)S(1)} concatenate(f32[1]{0:T(128)} %bitcast.54, f32[1]{0:T(128)} %bitcast.55, f32[1]{0:T(128)} %bitcast.56, f32[1]{0:T(128)} %bitcast.57, f32[1]{0:T(128)} %bitcast.59, f32[1]{0:T(128)} %bitcast.60, f32[1]{0:T(128)} %bitcast.61, f32[1]{0:T(128)} %bitcast.62, f32[1]{0:T(128)} %bitcast.63, f32[1]{0:T(128)} %bitcast.64, f32[1]{0:T(128)} %bitcast.65, ...), dimensions={0} | concatenate | bytes 104 | tf_op jit(solution)/shard_map/stack | solution.py:108
  401.8 29.3 %psum.60 = f32[13]{0:T(128)} all-reduce(f32[13]{0:T(128)S(1)} %stack.194), channel_id=1, replica_groups=mesh['row'=16,'col'=16] {'col'}, use_global_device_ids=true, to_apply=%region_28.0 | all-reduce | flops 13 | bytes 104 | tf_op jit(solution)/shard_map/psum | solution.py:17
  431.1 32.8 %psum.61 = f32[13]{0:T(128)S(1)} all-reduce(f32[13]{0:T(128)} %psum.60), channel_id=1, replica_groups=mesh['row'=16,'col'=16] {'row'}, use_global_device_ids=true, to_apply=%region_29.0 | all-reduce | flops 13 | bytes 104 | tf_op jit(solution)/shard_map/psum | solution.py:17
  496.8 6.0 fusion.73
  510.8 4.9 copy.75
  515.7 7.8 %convolution_bitcast_fusion.50 = f32[16,2,4,64,64]{4,3,2,1,0:T(8,128)} fusion(bf16[64,2,4,1024,1]{0,3,2,1,4:T(8,128)(2,1)S(1)} %bitcast.660, bf16[16,64,1024,1,1]{2,1,4,3,0:T(8,128)(2,1)} %bitcast.671), kind=kOutput, calls=%fused_computation.273 | convolution fusion | flops 1073741824 | bytes 5242880 | tf_op jit(solution)/shard_map/dot_general | solution.py:57
  523.4 5.5 reshape.707
  540.1 22.7 %all-to-all-done.2 = f32[16,1,32768]{2,1,0:T(1,128)} async-done(((f32[16,1,32768]{2,1,0:T(1,128)}), f32[16,1,32768]{2,1,0:T(1,128)}, u32[]{:S(2)}, u32[]{:S(2)}) %all-to-all-start.2) | async-done | bytes 2097184 | tf_op jit(solution)/shard_map/all_to_all | solution.py:65
  562.8 7.2 %reduce.50 = f32[16,32768]{1,0:T(8,128)S(1)} reduce(f32[16,1,32768]{2,1,0:T(1,128)} %all-to-all-done.2, f32[]{:T(128)} %broadcast.401), dimensions={1}, to_apply=%all_to_all.11.reduce_sub_computation | reduce | bytes 4194308 | tf_op jit(solution)/shard_map/all_to_all | solution.py:65
  576.6 5.8 stack.208
  582.5 28.8 %psum.62 = f32[9]{0:T(128)S(1)} all-reduce(f32[9]{0:T(128)S(1)} %stack.208), channel_id=1, replica_groups=mesh['row'=16,'col'=16] {'col'}, use_global_device_ids=true, to_apply=%region_45.0 | all-reduce | flops 9 | bytes 72 | tf_op jit(solution)/shard_map/psum | solution.py:17
  611.4 32.7 %psum.63 = f32[9]{0:T(128)S(1)} all-reduce(f32[9]{0:T(128)S(1)} %psum.62), channel_id=1, replica_groups=mesh['row'=16,'col'=16] {'row'}, use_global_device_ids=true, to_apply=%region_46.0 | all-reduce | flops 9 | bytes 72 | tf_op jit(solution)/shard_map/psum | solution.py:17
  (168 shorter events, 142.0 us)
Async XLA Ops:
  7.2 77.0 %all-gather.6.cloned.1.call-start = ((), (), s32[]{:S(2)}) async-start(), calls=%async_computation.3 | async-start | bytes 2228224 | tf_op jit(solution)/shard_map/all_gather | solution.py:75
  8.9 94.0 %all-gather.8.cloned.1.call-start = ((), (), s32[]{:S(2)}) async-start(), calls=%async_computation.4 | async-start | bytes 2228224 | tf_op jit(solution)/shard_map/all_gather | solution.py:41
  9.6 135.9 %all-gather.10.cloned.1.call-start = ((), (), s32[]{:S(2)}) async-start(), calls=%async_computation.5 | async-start | bytes 2228224 | tf_op jit(solution)/shard_map/all_gather | solution.py:42
  83.5 228.9 %copy-start.7 = (bf16[16,16,4,4,1,1]{0,1,2,3,5,4:T(8,128)(2,1)}, bf16[16,16,4,4,1,1]{0,1,2,3,5,4:T(8,128)(2,1)S(1)}, u32[]{:S(2)}) copy-start(bf16[16,16,4,4,1,1]{0,1,2,3,5,4:T(8,128)(2,1)S(1)} %copy.83) | copy-start | bytes 24580
  159.8 7.0 %copy-start = (bf16[64,4,64]{2,1,0:T(4,128)(2,1)S(1)}, bf16[64,4,64]{2,1,0:T(4,128)(2,1)}, u32[]{:S(2)}) copy-start(bf16[64,4,64]{2,1,0:T(4,128)(2,1)} %param.42) | copy-start | bytes 98308
  159.8 7.0 %copy-start.1 = (bf16[64,4,64]{2,1,0:T(4,128)(2,1)S(1)}, bf16[64,4,64]{2,1,0:T(4,128)(2,1)}, u32[]{:S(2)}) copy-start(bf16[64,4,64]{2,1,0:T(4,128)(2,1)} %param.43) | copy-start | bytes 98308
  159.8 36.0 %all-to-all-start = ((f32[16,1,32768]{2,1,0:T(1,128)}), f32[16,1,32768]{2,1,0:T(1,128)}, u32[]{:S(2)}, u32[]{:S(2)}) async-start(f32[16,1,32768]{2,1,0:T(1,128)} %reshape.703), calls=%async_computation | async-start | bytes 4194304 | tf_op jit(solution)/shard_map/all_to_all | solution.py:65
  166.5 125.9 %all-gather.12.cloned.1.call-start = ((), (), s32[]{:S(2)}) async-start(), calls=%async_computation.6 | async-start | bytes 4456448 | tf_op jit(solution)/shard_map/all_gather | solution.py:94
  209.0 2.7 copy-start.8
  211.8 85.1 %copy-start.4 = (f32[64,2,4,64]{3,0,2,1:T(8,128)}, f32[64,2,4,64]{3,0,2,1:T(8,128)S(1)}, u32[]{:S(2)}) copy-start(f32[64,2,4,64]{3,0,2,1:T(8,128)S(1)} %fusion.70) | copy-start | bytes 393220
  303.9 1.6 copy-start.5
  337.1 33.7 %all-to-all-start.1 = ((f32[16,1,32768]{2,1,0:T(1,128)}), f32[16,1,32768]{2,1,0:T(1,128)}, u32[]{:S(2)}, u32[]{:S(2)}) async-start(f32[16,1,32768]{2,1,0:T(1,128)} %reshape.705), calls=%async_computation.1 | async-start | bytes 4194304 | tf_op jit(solution)/shard_map/all_to_all | solution.py:65
  341.5 145.4 %all-gather.14.cloned.1.call-start = ((), (), s32[]{:S(2)}) async-start(), calls=%async_computation.7 | async-start | bytes 4456448 | tf_op jit(solution)/shard_map/all_gather | solution.py:94
  386.4 0.7 copy-start.2
  401.2 0.6 copy-start.10
  502.8 1.6 copy-start.6
  528.9 5.7 copy-start.9
  528.9 8.6 %copy-start.3 = (f32[64,2,4,64]{3,0,2,1:T(8,128)S(1)}, f32[64,2,4,64]{3,0,2,1:T(8,128)}, u32[]{:S(2)}) copy-start(f32[64,2,4,64]{3,0,2,1:T(8,128)} %copy-done.2) | copy-start | bytes 393220
  528.9 33.8 %all-to-all-start.2 = ((f32[16,1,32768]{2,1,0:T(1,128)}), f32[16,1,32768]{2,1,0:T(1,128)}, u32[]{:S(2)}, u32[]{:S(2)}) async-start(f32[16,1,32768]{2,1,0:T(1,128)} %reshape.707), calls=%async_computation.2 | async-start | bytes 4194304 | tf_op jit(solution)/shard_map/all_to_all | solution.py:65
  573.0 71.3 %copy-start.11 = (f32[3,1]{0,1:T(1,128)S(1)}, f32[3,1]{0,1:T(1,128)}, u32[]{:S(2)}) copy-start(f32[3,1]{0,1:T(1,128)} %constant.468) | copy-start | bytes 40
Sparse Core Ops, SparseCore 0:
  10.4 43.5 all-gather.5
  56.4 46.3 all-gather.7
  104.7 40.7 all-gather.9
  212.9 40.0 all-gather.11
  388.1 39.4 all-gather.13

commit v4 on v3

--- a/solution.py
+++ b/solution.py
@@ -54,15 +54,14 @@
         channel = channel.astype(jnp.bfloat16).reshape(
             rows_here * panels * physical, cols_here * channels
         )
-        partial_rows = lax.dot_general(
-            channel, right_whole, (((1,), (1,)), ((), ())), preferred_element_type=jnp.float32
+        partial_cols = lax.dot_general(
+            right_whole, channel, (((1,), (1,)), ((), ())), preferred_element_type=jnp.float32
         )
-        partial_rows = partial_rows.reshape(rows_here, panels, physical, partial_rows.shape[1])
         blocks = lax.psum(1, "col")
-        split = partial_rows.reshape(
-            rows_here, panels, physical, blocks, partial_rows.shape[3] // blocks
-        )
-        summed = jnp.sum(lax.all_to_all(split, "col", 3, 3, tiled=False), axis=3)
+        split = partial_cols.reshape(blocks, partial_cols.shape[0] // blocks, channel.shape[0])
+        gathered = lax.all_to_all(split, "col", 0, 0, tiled=False)
+        summed = jnp.sum(gathered, axis=0).reshape(cols_here, rows_here, panels, physical)
+        summed = jnp.transpose(summed, (1, 2, 3, 0))
         return summed - dissipation[None, None, :, None] * stacked
 
     primal = site_tensor.astype(jnp.float32)

time: 675 us -> 642 us (0.951); the launches traced: 665 us -> 639 us
  local copies, waits for them, and re-layouts: 132 us -> 163 us
  other arithmetic: 61.2 us -> 38 us
  waiting for transfers between devices: 111 us -> 91.2 us
  matrix products: 55.4 us -> 41.5 us
    reshape x0 -> x3, local copies, waits for them, and re-layouts: none -> 46.1 us  [apply(): channel.astype(jnp.bfloat16)]
    unnamed x37 -> x27, local copies, waits for them, and re-layouts: 44.6 us -> 15.2 us
    all_to_all x3 -> x0, other arithmetic: 24.4 us -> none  [apply(): summed = jnp.sum(lax.all_to_all(split, 'col', 3, 3, tiled=False), axis=3)]
    all_gather x1, waiting for transfers between devices: 16.6 us -> 0.02 us  [local(): right_whole = lax.all_gather(right_env, 'row', axis=0, tiled=True)]
    dot_general x3, matrix products: 25.2 us -> 11.5 us  [apply(): lax.dot_general(right_whole, channel, (((1,), (1,)), ((), ())), preferred...]
    dot_general x0 -> x3, local copies, waits for them, and re-layouts: none -> 7.77 us  [apply(): lax.dot_general(right_whole, channel, (((1,), (1,)), ((), ())), preferred...]
  transfers between devices with their start and end apart: 8 -> 8, of which waited for: 5 -> 4; matrix products, arithmetic and copies ran while one was open for 12% -> 15% of each run, Pallas kernels for 0% -> 0%
where the time goes in v4:
time: 642 us; the launch traced here: 639 us
  blocking collectives  255 us (40%)
  local copies, waits for them, and re-layouts  163 us (25%)
  waiting for transfers between devices  91.2 us (14%)
  matrix products  41.5 us (6%)
  other arithmetic  38 us (6%)
  between operations  35.2 us (5%)
  starting transfers between devices  14.6 us (2%)
    psum x8, blocking collectives, total(): return lax.psum(lax.psum(values, 'col'), 'row')  255 us
    all_to_all x3, waiting for transfers between devices, apply(): gathered = lax.all_to_all(split, 'col', 0, 0, tiled=False)  75.9 us
    reshape x3, local copies, waits for them, and re-layouts, apply(): channel.astype(jnp.bfloat16)  46.1 us
    convert_element_type x3, local copies, waits for them, and re-layouts, apply(): channel.astype(jnp.bfloat16)  21.5 us
    another operation x3, local copies, waits for them, and re-layouts, local(): totals = total(jnp.stack(locals_list))  18.6 us
    unnamed x27, local copies, waits for them, and re-layouts  15.2 us
    all_to_all x3, starting transfers between devices, apply(): gathered = lax.all_to_all(split, 'col', 0, 0, tiled=False)  14.4 us
    all_gather x1, waiting for transfers between devices, local(): left_whole = lax.all_gather(left_env, 'col', axis=1, tiled=True)  13.8 us
  transfers between devices with their start and end apart: 8, of which 4 were waited for; matrix products, arithmetic and copies ran while one was open for 15% of the time, Pallas kernels for 0%

profile of v4, /device:TPU:1, one launch (start us, length us, event | category | flops | bytes accessed | tf_op | source)
XLA Modules:
  0.0 639.1 jit_solution(1014243411635415323)
XLA Ops:
  13.4 34.2 %psum.56 = f32[2]{0:T(128)S(1)} all-reduce(f32[2]{0:T(128)S(1)} %pad_maximum_fusion.4), channel_id=1, replica_groups=mesh['row'=16,'col'=16] {'col'}, use_global_device_ids=true, to_apply=%region_2.0 | all-reduce | flops 2 | bytes 16 | tf_op jit(solution)/shard_map/psum | solution.py:17
  47.6 33.8 %psum.57 = f32[2]{0:T(128)S(1)} all-reduce(f32[2]{0:T(128)S(1)} %psum.56), channel_id=1, replica_groups=mesh['row'=16,'col'=16] {'row'}, use_global_device_ids=true, to_apply=%region_3.0 | all-reduce | flops 2 | bytes 16 | tf_op jit(solution)/shard_map/psum | solution.py:17
  89.1 13.8 %all-gather.8.cloned.1.call-done = bf16[64,16384]{1,0:T(8,128)(2,1)} async-done(((bf16[64,1024]{1,0:T(8,128)(2,1)}), bf16[64,16384]{1,0:T(8,128)(2,1)}) %all-gather.8.cloned.1.call-update) | async-done | bytes 2097168 | tf_op jit(solution)/shard_map/all_gather | solution.py:41
  102.9 4.8 copy.48
  107.7 5.5 copy.50
  118.5 4.7 fusion.3
  123.2 7.8 %copy.53 = bf16[64,2,4,64,16]{4,3,2,1,0:T(8,128)(2,1)} copy(bf16[64,2,4,64,16]{3,4,2,1,0:T(8,128)(2,1)} %fusion.3) | data formatting | bytes 2097152 | tf_op jit(solution)/shard_map/convert_element_type | solution.py:54
  131.0 15.2 %reshape.569 = bf16[512,1024]{1,0:T(8,128)(2,1)S(1)} reshape(bf16[64,2,4,64,16]{4,3,2,1,0:T(8,128)(2,1)} %copy.53) | data formatting | bytes 2097152 | tf_op jit(solution)/shard_map/reshape | solution.py:54
  153.3 6.1 all-to-all-start
  159.5 26.3 %all-to-all-done = f32[16,64,512]{2,1,0:T(8,128)} async-done(((f32[16,64,512]{2,1,0:T(8,128)}), f32[16,64,512]{2,1,0:T(8,128)}, u32[]{:S(2)}, u32[]{:S(2)}) %all-to-all-start) | async-done | bytes 2097184 | tf_op jit(solution)/shard_map/all_to_all | solution.py:62
  190.5 4.6 stack.176
  195.1 30.6 %psum.58 = f32[7]{0:T(128)S(1)} all-reduce(f32[7]{0:T(128)S(1)} %stack.176), channel_id=1, replica_groups=mesh['row'=16,'col'=16] {'col'}, use_global_device_ids=true, to_apply=%region_12.0 | all-reduce | flops 7 | bytes 56 | tf_op jit(solution)/shard_map/psum | solution.py:17
  225.7 33.2 %psum.59 = f32[7]{0:T(128)S(1)} all-reduce(f32[7]{0:T(128)S(1)} %psum.58), channel_id=1, replica_groups=mesh['row'=16,'col'=16] {'row'}, use_global_device_ids=true, to_apply=%region_13.0 | all-reduce | flops 7 | bytes 56 | tf_op jit(solution)/shard_map/psum | solution.py:17
  271.2 4.5 fusion.138
  286.6 4.7 reshape.577
  291.2 4.7 fusion.6
  296.0 7.8 %copy.64 = bf16[64,2,4,64,16]{4,3,2,1,0:T(8,128)(2,1)} copy(bf16[64,2,4,64,16]{3,4,2,1,0:T(8,128)(2,1)} %fusion.6) | data formatting | bytes 2097152 | tf_op jit(solution)/shard_map/convert_element_type | solution.py:54
  303.8 15.8 %reshape.578 = bf16[512,1024]{1,0:T(8,128)(2,1)} reshape(bf16[64,2,4,64,16]{4,3,2,1,0:T(8,128)(2,1)} %copy.64) | data formatting | bytes 2097152 | tf_op jit(solution)/shard_map/reshape | solution.py:54
  319.6 4.5 convolution_bitcast_fusion.1
  333.8 26.9 %all-to-all-done.1 = f32[16,64,512]{2,1,0:T(8,128)} async-done(((f32[16,64,512]{2,1,0:T(8,128)}), f32[16,64,512]{2,1,0:T(8,128)}, u32[]{:S(2)}, u32[]{:S(2)}) %all-to-all-start.1) | async-done | bytes 2097184 | tf_op jit(solution)/shard_map/all_to_all | solution.py:62
  372.3 8.2 %stack.194 = f32[13]{0:T(128)S(1)} concatenate(f32[1]{0:T(128)} %bitcast.53, f32[1]{0:T(128)} %bitcast.54, f32[1]{0:T(128)} %bitcast.55, f32[1]{0:T(128)} %bitcast.56, f32[1]{0:T(128)} %bitcast.58, f32[1]{0:T(128)} %bitcast.59, f32[1]{0:T(128)} %bitcast.60, f32[1]{0:T(128)} %bitcast.61, f32[1]{0:T(128)} %bitcast.62, f32[1]{0:T(128)} %bitcast.63, f32[1]{0:T(128)} %bitcast.64, ...), dimensions={0} | concatenate | bytes 104 | tf_op jit(solution)/shard_map/stack | solution.py:107
  381.8 29.4 %psum.60 = f32[13]{0:T(128)} all-reduce(f32[13]{0:T(128)S(1)} %stack.194), channel_id=1, replica_groups=mesh['row'=16,'col'=16] {'col'}, use_global_device_ids=true, to_apply=%region_28.0 | all-reduce | flops 13 | bytes 104 | tf_op jit(solution)/shard_map/psum | solution.py:17
  411.2 32.8 %psum.61 = f32[13]{0:T(128)S(1)} all-reduce(f32[13]{0:T(128)} %psum.60), channel_id=1, replica_groups=mesh['row'=16,'col'=16] {'row'}, use_global_device_ids=true, to_apply=%region_29.0 | all-reduce | flops 13 | bytes 104 | tf_op jit(solution)/shard_map/psum | solution.py:17
  467.9 4.5 fusion.137
  477.8 6.0 fusion.72
  492.2 5.9 copy.76
  498.2 15.1 %reshape.591 = bf16[512,1024]{1,0:T(8,128)(2,1)S(1)} reshape(bf16[64,2,4,64,16]{4,3,2,1,0:T(8,128)(2,1)} %copy.76) | data formatting | bytes 2097152 | tf_op jit(solution)/shard_map/reshape | solution.py:54
  528.4 22.7 %all-to-all-done.2 = f32[16,64,512]{2,1,0:T(8,128)S(1)} async-done(((f32[16,64,512]{2,1,0:T(8,128)}), f32[16,64,512]{2,1,0:T(8,128)S(1)}, u32[]{:S(2)}, u32[]{:S(2)}) %all-to-all-start.2) | async-done | bytes 2097184 | tf_op jit(solution)/shard_map/all_to_all | solution.py:62
  552.6 5.8 stack.208
  558.5 28.8 %psum.62 = f32[9]{0:T(128)S(1)} all-reduce(f32[9]{0:T(128)S(1)} %stack.208), channel_id=1, replica_groups=mesh['row'=16,'col'=16] {'col'}, use_global_device_ids=true, to_apply=%region_45.0 | all-reduce | flops 9 | bytes 72 | tf_op jit(solution)/shard_map/psum | solution.py:17
  587.4 32.6 %psum.63 = f32[9]{0:T(128)S(1)} all-reduce(f32[9]{0:T(128)S(1)} %psum.62), channel_id=1, replica_groups=mesh['row'=16,'col'=16] {'row'}, use_global_device_ids=true, to_apply=%region_46.0 | all-reduce | flops 9 | bytes 72 | tf_op jit(solution)/shard_map/psum | solution.py:17
  628.0 4.5 multiply_add_fusion
  (162 shorter events, 118.1 us)
Async XLA Ops:
  7.2 77.3 %all-gather.6.cloned.1.call-start = ((), (), s32[]{:S(2)}) async-start(), calls=%async_computation.3 | async-start | bytes 2228224 | tf_op jit(solution)/shard_map/all_gather | solution.py:74
  8.9 94.0 %all-gather.8.cloned.1.call-start = ((), (), s32[]{:S(2)}) async-start(), calls=%async_computation.4 | async-start | bytes 2228224 | tf_op jit(solution)/shard_map/all_gather | solution.py:41
  9.6 136.6 %all-gather.10.cloned.1.call-start = ((), (), s32[]{:S(2)}) async-start(), calls=%async_computation.5 | async-start | bytes 2228224 | tf_op jit(solution)/shard_map/all_gather | solution.py:42
  153.3 6.1 copy-start
  153.3 6.2 copy-start.6
  153.3 32.5 %all-to-all-start = ((f32[16,64,512]{2,1,0:T(8,128)}), f32[16,64,512]{2,1,0:T(8,128)}, u32[]{:S(2)}, u32[]{:S(2)}) async-start(f32[16,64,512]{2,1,0:T(8,128)} %bitcast.663), calls=%async_computation | async-start | bytes 4194304 | tf_op jit(solution)/shard_map/all_to_all | solution.py:62
  159.4 28.3 %copy-start.7 = (f32[4]{0:T(128)S(1)}, f32[4]{0:T(128)}, u32[]{:S(2)}) copy-start(f32[4]{0:T(128)} %param.47) | copy-start | bytes 52
  159.4 111.8 %all-gather.12.cloned.1.call-start = ((), (), s32[]{:S(2)}) async-start(), calls=%async_computation.6 | async-start | bytes 4456448 | tf_op jit(solution)/shard_map/all_gather | solution.py:93
  282.6 1.6 copy-start.4
  327.0 33.7 %all-to-all-start.1 = ((f32[16,64,512]{2,1,0:T(8,128)}), f32[16,64,512]{2,1,0:T(8,128)}, u32[]{:S(2)}, u32[]{:S(2)}) async-start(f32[16,64,512]{2,1,0:T(8,128)} %bitcast.662), calls=%async_computation.1 | async-start | bytes 4194304 | tf_op jit(solution)/shard_map/all_to_all | solution.py:62
  331.5 136.5 %all-gather.14.cloned.1.call-start = ((), (), s32[]{:S(2)}) async-start(), calls=%async_computation.7 | async-start | bytes 4456448 | tf_op jit(solution)/shard_map/all_gather | solution.py:93
  366.0 0.7 copy-start.2
  381.2 0.6 copy-start.9
  483.8 1.6 copy-start.5
  518.1 4.7 copy-start.8
  518.1 7.7 %copy-start.1 = (f32[64,4,64]{2,1,0:T(4,128)S(1)}, f32[64,4,64]{2,1,0:T(4,128)}, u32[]{:S(2)}) copy-start(f32[64,4,64]{2,1,0:T(4,128)} %get-tuple-element.269) | copy-start | bytes 196612
  518.1 7.7 %copy-start.3 = (f32[64,2,4,64]{3,2,0,1:T(4,128)S(1)}, f32[64,2,4,64]{3,2,0,1:T(4,128)}, u32[]{:S(2)}) copy-start(f32[64,2,4,64]{3,2,0,1:T(4,128)} %copy-done.2) | copy-start | bytes 393220
  518.1 33.1 %all-to-all-start.2 = ((f32[16,64,512]{2,1,0:T(8,128)}), f32[16,64,512]{2,1,0:T(8,128)S(1)}, u32[]{:S(2)}, u32[]{:S(2)}) async-start(f32[16,64,512]{2,1,0:T(8,128)} %bitcast.661), calls=%async_computation.2 | async-start | bytes 4194304 | tf_op jit(solution)/shard_map/all_to_all | solution.py:62
  528.4 91.9 %copy-start.10 = (f32[3,1]{0,1:T(1,128)S(1)}, f32[3,1]{0,1:T(1,128)}, u32[]{:S(2)}) copy-start(f32[3,1]{0,1:T(1,128)} %constant.468) | copy-start | bytes 40
Sparse Core Ops, SparseCore 0:
  10.4 43.5 all-gather.5
  56.4 46.3 all-gather.7
  104.7 40.7 all-gather.9
  188.7 43.1 all-gather.11
  367.6 41.2 all-gather.13

commit v5 on v4

--- a/solution.py
+++ b/solution.py
@@ -40,6 +40,9 @@
     channels = mpo.shape[0]
     left_whole = lax.all_gather(left_env, "col", axis=1, tiled=True)
     right_whole = lax.all_gather(right_env, "row", axis=0, tiled=True)
+    right_whole = jnp.transpose(
+        right_whole.reshape(right_whole.shape[0], cols_here, channels), (0, 2, 1)
+    ).reshape(right_whole.shape[0], channels * cols_here)
 
     def apply(stacked, whole_stacked):
         panels = stacked.shape[1]
@@ -50,7 +53,7 @@
             left_three, flat, (((1,), (0,)), ((), ())), preferred_element_type=jnp.float32
         )
         mixed = mixed.astype(jnp.bfloat16).reshape(rows_here, channels, panels, physical, cols_here)
-        channel = jnp.einsum("awspr,wvpq->asqrv", mixed, mpo, preferred_element_type=jnp.float32)
+        channel = jnp.einsum("awspr,wvpq->asqvr", mixed, mpo, preferred_element_type=jnp.float32)
         channel = channel.astype(jnp.bfloat16).reshape(
             rows_here * panels * physical, cols_here * channels
         )

time: 642 us -> 609 us (0.949)
  local copies, waits for them, and re-layouts: 163 us -> 113 us
  waiting for transfers between devices: 91.2 us -> 114 us
    reshape x3, local copies, waits for them, and re-layouts: 46.1 us -> 10.7 us  [apply(): channel.astype(jnp.bfloat16)]
    convert_element_type x3 -> x0, local copies, waits for them, and re-layouts: 21.5 us -> none  [apply(): channel.astype(jnp.bfloat16)]
    all_gather x1, waiting for transfers between devices: 0.02 us -> 19.1 us  [local(): right_whole = lax.all_gather(right_env, 'row', axis=0, tiled=True)]
    unnamed x27 -> x31, local copies, waits for them, and re-layouts: 15.2 us -> 16.6 us
  transfers between devices with their start and end apart: 8 -> 8, of which waited for: 4 -> 5; matrix products, arithmetic and copies ran while one was open for 15% -> 13% of each run, Pallas kernels for 0% -> 0%
where the time goes in v5:
time: 609 us; the launch traced here: 607 us
  blocking collectives  253 us (42%)
  waiting for transfers between devices  114 us (19%)
  local copies, waits for them, and re-layouts  113 us (19%)
  matrix products  39 us (6%)
  other arithmetic  37.8 us (6%)
  between operations  34.4 us (6%)
  starting transfers between devices  15.2 us (2%)
    psum x8, blocking collectives, total(): return lax.psum(lax.psum(values, 'col'), 'row')  253 us
    all_to_all x3, waiting for transfers between devices, apply(): gathered = lax.all_to_all(split, 'col', 0, 0, tiled=False)  79.1 us
    all_gather x1, waiting for transfers between devices, local(): right_whole = lax.all_gather(right_env, 'row', axis=0, tiled=True)  19.1 us
    another operation x3, local copies, waits for them, and re-layouts, local(): totals = total(jnp.stack(locals_list))  18.1 us
    unnamed x31, local copies, waits for them, and re-layouts  16.6 us
    all_to_all x3, starting transfers between devices, apply(): gathered = lax.all_to_all(split, 'col', 0, 0, tiled=False)  15 us
    all_gather x1, waiting for transfers between devices, local(): left_whole = lax.all_gather(left_env, 'col', axis=1, tiled=True)  14 us
    dot_general x3, matrix products, apply(): jnp.einsum('awspr,wvpq->asqvr', mixed, mpo, preferred_element_type=jnp.fl...  12.5 us
  transfers between devices with their start and end apart: 8, of which 5 were waited for; matrix products, arithmetic and copies ran while one was open for 13% of the time, Pallas kernels for 0%

profile of v5, /device:TPU:1, one launch (start us, length us, event | category | flops | bytes accessed | tf_op | source)
XLA Modules:
  0.0 606.6 jit_solution(6004869786806877603)
XLA Ops:
  13.3 34.2 %psum.56 = f32[2]{0:T(128)S(1)} all-reduce(f32[2]{0:T(128)S(1)} %pad_maximum_fusion.4), channel_id=1, replica_groups=mesh['row'=16,'col'=16] {'col'}, use_global_device_ids=true, to_apply=%region_2.0 | all-reduce | flops 2 | bytes 16 | tf_op jit(solution)/shard_map/psum | solution.py:17
  47.5 33.8 %psum.57 = f32[2]{0:T(128)S(1)} all-reduce(f32[2]{0:T(128)S(1)} %psum.56), channel_id=1, replica_groups=mesh['row'=16,'col'=16] {'row'}, use_global_device_ids=true, to_apply=%region_3.0 | all-reduce | flops 2 | bytes 16 | tf_op jit(solution)/shard_map/psum | solution.py:17
  88.8 14.0 %all-gather.8.cloned.1.call-done = bf16[64,16384]{1,0:T(8,128)(2,1)} async-done(((bf16[64,1024]{1,0:T(8,128)(2,1)}), bf16[64,16384]{1,0:T(8,128)(2,1)}) %all-gather.8.cloned.1.call-update) | async-done | bytes 2097168 | tf_op jit(solution)/shard_map/all_gather | solution.py:41
  102.9 4.8 copy.47
  107.7 5.5 copy.49
  118.5 4.7 fusion.3
  126.4 19.1 %all-gather.10.cloned.1.call-done = bf16[1024,1024]{1,0:T(8,128)(2,1)} async-done(((bf16[64,1024]{1,0:T(8,128)(2,1)}), bf16[1024,1024]{1,0:T(8,128)(2,1)}) %all-gather.10.cloned.1.call-update) | async-done | bytes 2097168 | tf_op jit(solution)/shard_map/all_gather | solution.py:42
  145.5 4.0 copy.52
  159.1 6.7 %all-to-all-start = ((f32[16,64,512]{2,1,0:T(8,128)}), f32[16,64,512]{2,1,0:T(8,128)}, u32[]{:S(2)}, u32[]{:S(2)}) async-start(f32[16,64,512]{2,1,0:T(8,128)} %bitcast.667), calls=%async_computation | async-start | bytes 4194304 | tf_op jit(solution)/shard_map/all_to_all | solution.py:65
  166.0 29.1 %all-to-all-done = f32[16,64,512]{2,1,0:T(8,128)} async-done(((f32[16,64,512]{2,1,0:T(8,128)}), f32[16,64,512]{2,1,0:T(8,128)}, u32[]{:S(2)}, u32[]{:S(2)}) %all-to-all-start) | async-done | bytes 2097184 | tf_op jit(solution)/shard_map/all_to_all | solution.py:65
  199.7 4.3 stack.176
  204.0 29.0 %psum.58 = f32[7]{0:T(128)S(1)} all-reduce(f32[7]{0:T(128)S(1)} %stack.176), channel_id=1, replica_groups=mesh['row'=16,'col'=16] {'col'}, use_global_device_ids=true, to_apply=%region_12.0 | all-reduce | flops 7 | bytes 56 | tf_op jit(solution)/shard_map/psum | solution.py:17
  233.0 32.6 %psum.59 = f32[7]{0:T(128)S(1)} all-reduce(f32[7]{0:T(128)S(1)} %psum.58), channel_id=1, replica_groups=mesh['row'=16,'col'=16] {'row'}, use_global_device_ids=true, to_apply=%region_13.0 | all-reduce | flops 7 | bytes 56 | tf_op jit(solution)/shard_map/psum | solution.py:17
  277.9 4.5 fusion.138
  293.2 4.7 reshape.585
  297.9 4.7 fusion.6
  302.5 4.1 reshape.586
  306.6 4.5 convolution_bitcast_fusion.1
  314.1 4.4 all-to-all-start.1
  320.8 26.9 %all-to-all-done.1 = f32[16,64,512]{2,1,0:T(8,128)} async-done(((f32[16,64,512]{2,1,0:T(8,128)}), f32[16,64,512]{2,1,0:T(8,128)}, u32[]{:S(2)}, u32[]{:S(2)}) %all-to-all-start.1) | async-done | bytes 2097184 | tf_op jit(solution)/shard_map/all_to_all | solution.py:65
  359.4 8.1 %stack.194 = f32[13]{0:T(128)S(1)} concatenate(f32[1]{0:T(128)} %bitcast.56, f32[1]{0:T(128)} %bitcast.57, f32[1]{0:T(128)} %bitcast.58, f32[1]{0:T(128)} %bitcast.59, f32[1]{0:T(128)} %bitcast.61, f32[1]{0:T(128)} %bitcast.62, f32[1]{0:T(128)} %bitcast.63, f32[1]{0:T(128)} %bitcast.64, f32[1]{0:T(128)} %bitcast.65, f32[1]{0:T(128)} %bitcast.66, f32[1]{0:T(128)} %bitcast.67, ...), dimensions={0} | concatenate | bytes 104 | tf_op jit(solution)/shard_map/stack | solution.py:110
  368.8 29.3 %psum.60 = f32[13]{0:T(128)} all-reduce(f32[13]{0:T(128)S(1)} %stack.194), channel_id=1, replica_groups=mesh['row'=16,'col'=16] {'col'}, use_global_device_ids=true, to_apply=%region_28.0 | all-reduce | flops 13 | bytes 104 | tf_op jit(solution)/shard_map/psum | solution.py:17
  398.1 32.8 %psum.61 = f32[13]{0:T(128)S(1)} all-reduce(f32[13]{0:T(128)} %psum.60), channel_id=1, replica_groups=mesh['row'=16,'col'=16] {'row'}, use_global_device_ids=true, to_apply=%region_29.0 | all-reduce | flops 13 | bytes 104 | tf_op jit(solution)/shard_map/psum | solution.py:17
  453.8 4.5 fusion.137
  463.7 6.0 fusion.72
  476.8 3.4 reshape.599
  485.7 3.9 all-to-all-start.2
  495.8 23.0 %all-to-all-done.2 = f32[16,64,512]{2,1,0:T(8,128)S(1)} async-done(((f32[16,64,512]{2,1,0:T(8,128)}), f32[16,64,512]{2,1,0:T(8,128)S(1)}, u32[]{:S(2)}, u32[]{:S(2)}) %all-to-all-start.2) | async-done | bytes 2097184 | tf_op jit(solution)/shard_map/all_to_all | solution.py:65
  520.2 5.6 stack.208
  526.0 28.8 %psum.62 = f32[9]{0:T(128)S(1)} all-reduce(f32[9]{0:T(128)S(1)} %stack.208), channel_id=1, replica_groups=mesh['row'=16,'col'=16] {'col'}, use_global_device_ids=true, to_apply=%region_45.0 | all-reduce | flops 9 | bytes 72 | tf_op jit(solution)/shard_map/psum | solution.py:17
  554.9 32.7 %psum.63 = f32[9]{0:T(128)S(1)} all-reduce(f32[9]{0:T(128)S(1)} %psum.62), channel_id=1, replica_groups=mesh['row'=16,'col'=16] {'row'}, use_global_device_ids=true, to_apply=%region_46.0 | all-reduce | flops 9 | bytes 72 | tf_op jit(solution)/shard_map/psum | solution.py:17
  595.5 4.5 multiply_add_fusion
  (165 shorter events, 113.9 us)
Async XLA Ops:
  7.2 77.1 %all-gather.6.cloned.1.call-start = ((), (), s32[]{:S(2)}) async-start(), calls=%async_computation.3 | async-start | bytes 2228224 | tf_op jit(solution)/shard_map/all_gather | solution.py:77
  8.9 94.0 %all-gather.8.cloned.1.call-start = ((), (), s32[]{:S(2)}) async-start(), calls=%async_computation.4 | async-start | bytes 2228224 | tf_op jit(solution)/shard_map/all_gather | solution.py:41
  9.6 135.9 %all-gather.10.cloned.1.call-start = ((), (), s32[]{:S(2)}) async-start(), calls=%async_computation.5 | async-start | bytes 2228224 | tf_op jit(solution)/shard_map/all_gather | solution.py:42
  152.2 1.3 copy-start.6
  159.1 6.8 %copy-start = (bf16[64,4,64]{2,1,0:T(4,128)(2,1)S(1)}, bf16[64,4,64]{2,1,0:T(4,128)(2,1)}, u32[]{:S(2)}) copy-start(bf16[64,4,64]{2,1,0:T(4,128)(2,1)} %param.42) | copy-start | bytes 98308
  159.1 6.8 %copy-start.8 = (bf16[64,4,64]{2,1,0:T(4,128)(2,1)S(1)}, bf16[64,4,64]{2,1,0:T(4,128)(2,1)}, u32[]{:S(2)}) copy-start(bf16[64,4,64]{2,1,0:T(4,128)(2,1)} %param.43) | copy-start | bytes 98308
  159.1 36.0 %all-to-all-start = ((f32[16,64,512]{2,1,0:T(8,128)}), f32[16,64,512]{2,1,0:T(8,128)}, u32[]{:S(2)}, u32[]{:S(2)}) async-start(f32[16,64,512]{2,1,0:T(8,128)} %bitcast.667), calls=%async_computation | async-start | bytes 4194304 | tf_op jit(solution)/shard_map/all_to_all | solution.py:65
  165.8 31.2 %copy-start.9 = (f32[4]{0:T(128)S(1)}, f32[4]{0:T(128)}, u32[]{:S(2)}) copy-start(f32[4]{0:T(128)} %param.47) | copy-start | bytes 52
  165.8 112.0 %all-gather.12.cloned.1.call-start = ((), (), s32[]{:S(2)}) async-start(), calls=%async_computation.6 | async-start | bytes 4456448 | tf_op jit(solution)/shard_map/all_gather | solution.py:96
  289.3 1.6 copy-start.4
  314.1 33.7 %all-to-all-start.1 = ((f32[16,64,512]{2,1,0:T(8,128)}), f32[16,64,512]{2,1,0:T(8,128)}, u32[]{:S(2)}, u32[]{:S(2)}) async-start(f32[16,64,512]{2,1,0:T(8,128)} %bitcast.666), calls=%async_computation.1 | async-start | bytes 4194304 | tf_op jit(solution)/shard_map/all_to_all | solution.py:65
  318.5 135.3 %all-gather.14.cloned.1.call-start = ((), (), s32[]{:S(2)}) async-start(), calls=%async_computation.7 | async-start | bytes 4456448 | tf_op jit(solution)/shard_map/all_gather | solution.py:96
  353.1 0.7 copy-start.2
  368.3 0.6 copy-start.11
  469.7 1.6 copy-start.5
  476.8 3.4 copy-start.7
  485.7 4.7 copy-start.10
  485.7 7.4 %copy-start.1 = (f32[64,4,64]{2,1,0:T(4,128)S(1)}, f32[64,4,64]{2,1,0:T(4,128)}, u32[]{:S(2)}) copy-start(f32[64,4,64]{2,1,0:T(4,128)} %get-tuple-element.269) | copy-start | bytes 196612
  485.7 7.4 %copy-start.3 = (f32[64,2,4,64]{3,2,0,1:T(4,128)S(1)}, f32[64,2,4,64]{3,2,0,1:T(4,128)}, u32[]{:S(2)}) copy-start(f32[64,2,4,64]{3,2,0,1:T(4,128)} %copy-done.2) | copy-start | bytes 393220
  485.7 33.1 %all-to-all-start.2 = ((f32[16,64,512]{2,1,0:T(8,128)}), f32[16,64,512]{2,1,0:T(8,128)S(1)}, u32[]{:S(2)}, u32[]{:S(2)}) async-start(f32[16,64,512]{2,1,0:T(8,128)} %bitcast.665), calls=%async_computation.2 | async-start | bytes 4194304 | tf_op jit(solution)/shard_map/all_to_all | solution.py:65
  495.8 92.0 %copy-start.12 = (f32[3,1]{0,1:T(1,128)S(1)}, f32[3,1]{0,1:T(1,128)}, u32[]{:S(2)}) copy-start(f32[3,1]{0,1:T(1,128)} %constant.468) | copy-start | bytes 40
Sparse Core Ops, SparseCore 0:
  10.4 43.5 all-gather.5
  56.4 46.3 all-gather.7
  104.7 40.7 all-gather.9
  198.0 39.9 all-gather.11
  354.7 39.6 all-gather.13

commit v6 on v5

--- a/solution.py
+++ b/solution.py
@@ -13,8 +13,14 @@
     return jnp.sum(first * second)
 
 
+def exchange_sum(values, axis):
+    size = lax.psum(1, axis)
+    copies = jnp.broadcast_to(values[None], (size,) + values.shape)
+    return jnp.sum(lax.all_to_all(copies, axis, 0, 0, tiled=False), axis=0)
+
+
 def total(values):
-    return lax.psum(lax.psum(values, "col"), "row")
+    return exchange_sum(exchange_sum(values, "col"), "row")
 
 
 def taylor(hess, dhess):

time: 609 us -> 499 us (0.82)
  blocking collectives: 253 us -> 59.8 us
  waiting for transfers between devices: 114 us -> 166 us
  starting transfers between devices: 15.2 us -> 40.6 us
    psum x8 -> x0, blocking collectives: 253 us -> none  [total(): return lax.psum(lax.psum(values, 'col'), 'row')]
    all_to_all x0 -> x5, blocking collectives: none -> 59.8 us  [exchange_sum(): return jnp.sum(lax.all_to_all(copies, axis, 0, 0, tiled=False), axis=0)]
    all_gather x1, waiting for transfers between devices: 14 us -> 44.2 us  [local(): left_whole = lax.all_gather(left_env, 'col', axis=1, tiled=True)]
    all_to_all x0 -> x3, starting transfers between devices: none -> 25.3 us  [exchange_sum(): return jnp.sum(lax.all_to_all(copies, axis, 0, 0, tiled=False), axis=0)]
    all_to_all x0 -> x3, waiting for transfers between devices: none -> 11.7 us  [exchange_sum(): return jnp.sum(lax.all_to_all(copies, axis, 0, 0, tiled=False), axis=0)]
    all_gather x1, waiting for transfers between devices: 0.02 us -> 6.78 us  [local(): lax.all_gather(jnp.stack([site_tensor, site_tangent], axis=1), 'row', axi...]
    unnamed x31 -> x29, local copies, waits for them, and re-layouts: 16.6 us -> 16.5 us
  transfers between devices with their start and end apart: 8 -> 11, of which waited for: 5 -> 9; matrix products, arithmetic and copies ran while one was open for 13% -> 17% of each run, Pallas kernels for 0% -> 0%
where the time goes in v6:
time: 499 us; the launch traced here: 496 us
  waiting for transfers between devices  166 us (33%)
  local copies, waits for them, and re-layouts  118 us (24%)
  blocking collectives  59.8 us (12%)
  starting transfers between devices  40.6 us (8%)
  matrix products  39.6 us (8%)
  other arithmetic  38.1 us (8%)
  between operations  34.4 us (7%)
    all_to_all x3, waiting for transfers between devices, apply(): gathered = lax.all_to_all(split, 'col', 0, 0, tiled=False)  82.6 us
    all_to_all x5, blocking collectives, exchange_sum(): return jnp.sum(lax.all_to_all(copies, axis, 0, 0, tiled=False), axis=0)  59.8 us
    all_gather x1, waiting for transfers between devices, local(): left_whole = lax.all_gather(left_env, 'col', axis=1, tiled=True)  44.2 us
    all_to_all x3, starting transfers between devices, exchange_sum(): return jnp.sum(lax.all_to_all(copies, axis, 0, 0, tiled=False), axis=0)  25.3 us
    all_gather x1, waiting for transfers between devices, local(): right_whole = lax.all_gather(right_env, 'row', axis=0, tiled=True)  19.1 us
    another operation x3, local copies, waits for them, and re-layouts, local(): totals = total(jnp.stack(locals_list))  18 us
    unnamed x29, local copies, waits for them, and re-layouts  16.5 us
    all_to_all x3, starting transfers between devices, apply(): gathered = lax.all_to_all(split, 'col', 0, 0, tiled=False)  15 us
  transfers between devices with their start and end apart: 11, of which 9 were waited for; matrix products, arithmetic and copies ran while one was open for 17% of the time, Pallas kernels for 0%

profile of v6, /device:TPU:1, one launch (start us, length us, event | category | flops | bytes accessed | tf_op | source)
XLA Modules:
  0.0 496.3 jit_solution(3735955625779128949)
XLA Ops:
  13.3 13.8 %all_to_all.63 = f32[16,1,2]{2,1,0:T(1,128)S(1)} all-to-all(f32[16,1,2]{2,1,0:T(1,128)S(1)} %broadcast_in_dim.16), channel_id=1, replica_groups=mesh['row'=16,'col'=16] {'col'}, dimensions={0} | all-to-all | bytes 256 | tf_op jit(solution)/shard_map/all_to_all | solution.py:19
  27.7 10.6 %all-to-all-start.1 = ((f32[16,1,2]{2,1,0:T(1,128)}), f32[16,1,2]{2,1,0:T(1,128)S(1)}, u32[]{:S(2)}, u32[]{:S(2)}) async-start(f32[16,1,2]{2,1,0:T(1,128)} %broadcast_in_dim.17), calls=%async_computation.1 | async-start | bytes 16384 | tf_op jit(solution)/shard_map/all_to_all | solution.py:19
  39.3 6.0 %all-to-all-done.1 = f32[16,1,2]{2,1,0:T(1,128)S(1)} async-done(((f32[16,1,2]{2,1,0:T(1,128)}), f32[16,1,2]{2,1,0:T(1,128)S(1)}, u32[]{:S(2)}, u32[]{:S(2)}) %all-to-all-start.1) | async-done | bytes 160 | tf_op jit(solution)/shard_map/all_to_all | solution.py:19
  47.3 6.8 %all-gather.6.cloned.1.call-done = bf16[1024,2,4,64]{3,2,1,0:T(4,128)(2,1)} async-done(((bf16[64,2,4,64]{3,2,1,0:T(4,128)(2,1)}), bf16[1024,2,4,64]{3,2,1,0:T(4,128)(2,1)}) %all-gather.6.cloned.1.call-update) | async-done | bytes 1048592 | tf_op jit(solution)/shard_map/all_gather | solution.py:83
  58.7 44.2 %all-gather.8.cloned.1.call-done = bf16[64,16384]{1,0:T(8,128)(2,1)} async-done(((bf16[64,1024]{1,0:T(8,128)(2,1)}), bf16[64,16384]{1,0:T(8,128)(2,1)}) %all-gather.8.cloned.1.call-update) | async-done | bytes 2097168 | tf_op jit(solution)/shard_map/all_gather | solution.py:47
  102.9 4.8 copy.153
  107.7 5.5 %copy.155 = bf16[64,1024,16]{1,0,2:T(8,128)(2,1)} copy(bf16[64,1024,16]{0,2,1:T(8,128)(2,1)} %bitcast.662) | data formatting | bytes 4194304 | tf_op jit(solution)/shard_map/reshape | solution.py:57
  118.5 4.7 fusion.3
  126.4 19.1 %all-gather.10.cloned.1.call-done = bf16[1024,1024]{1,0:T(8,128)(2,1)} async-done(((bf16[64,1024]{1,0:T(8,128)(2,1)}), bf16[1024,1024]{1,0:T(8,128)(2,1)}) %all-gather.10.cloned.1.call-update) | async-done | bytes 2097168 | tf_op jit(solution)/shard_map/all_gather | solution.py:48
  145.5 4.0 copy.158
  159.1 6.7 %all-to-all-start.2 = ((f32[16,64,512]{2,1,0:T(8,128)}), f32[16,64,512]{2,1,0:T(8,128)}, u32[]{:S(2)}, u32[]{:S(2)}) async-start(f32[16,64,512]{2,1,0:T(8,128)} %bitcast.667), calls=%async_computation.2 | async-start | bytes 4194304 | tf_op jit(solution)/shard_map/all_to_all | solution.py:71
  166.0 29.1 %all-to-all-done.2 = f32[16,64,512]{2,1,0:T(8,128)} async-done(((f32[16,64,512]{2,1,0:T(8,128)}), f32[16,64,512]{2,1,0:T(8,128)}, u32[]{:S(2)}, u32[]{:S(2)}) %all-to-all-start.2) | async-done | bytes 2097184 | tf_op jit(solution)/shard_map/all_to_all | solution.py:71
  199.7 4.3 stack.176
  204.0 11.1 %all_to_all.64 = f32[16,1,7]{2,1,0:T(1,128)S(1)} all-to-all(f32[16,1,7]{2,1,0:T(1,128)S(1)} %broadcast_in_dim.18), channel_id=1, replica_groups=mesh['row'=16,'col'=16] {'col'}, dimensions={0} | all-to-all | bytes 896 | tf_op jit(solution)/shard_map/all_to_all | solution.py:19
  215.2 14.0 %all_to_all.65 = f32[16,1,7]{2,1,0:T(1,128)S(1)} all-to-all(f32[16,1,7]{2,1,0:T(1,128)S(1)} %broadcast_in_dim.19), channel_id=1, replica_groups=mesh['row'=16,'col'=16] {'row'}, dimensions={0} | all-to-all | bytes 896 | tf_op jit(solution)/shard_map/all_to_all | solution.py:19
  241.4 4.5 fusion.138
  256.8 4.7 reshape.633
  261.4 4.7 fusion.6
  266.1 4.1 reshape.634
  270.2 4.5 convolution_bitcast_fusion.1
  277.6 4.4 all-to-all-start.5
  284.4 27.0 %all-to-all-done.5 = f32[16,64,512]{2,1,0:T(8,128)} async-done(((f32[16,64,512]{2,1,0:T(8,128)}), f32[16,64,512]{2,1,0:T(8,128)}, u32[]{:S(2)}, u32[]{:S(2)}) %all-to-all-start.5) | async-done | bytes 2097184 | tf_op jit(solution)/shard_map/all_to_all | solution.py:71
  320.3 7.9 %stack.194 = f32[13]{0:T(128)S(1)} concatenate(f32[1]{0:T(128)} %bitcast.56, f32[1]{0:T(128)} %bitcast.57, f32[1]{0:T(128)} %bitcast.58, f32[1]{0:T(128)} %bitcast.59, f32[1]{0:T(128)} %bitcast.61, f32[1]{0:T(128)} %bitcast.62, f32[1]{0:T(128)} %bitcast.63, f32[1]{0:T(128)} %bitcast.64, f32[1]{0:T(128)} %bitcast.65, f32[1]{0:T(128)} %bitcast.66, f32[1]{0:T(128)} %bitcast.67, ...), dimensions={0} | concatenate | bytes 104 | tf_op jit(solution)/shard_map/stack | solution.py:116
  328.3 10.5 %all_to_all.66 = f32[16,1,13]{2,1,0:T(1,128)S(1)} all-to-all(f32[16,1,13]{2,1,0:T(1,128)S(1)} %broadcast_in_dim.20), channel_id=1, replica_groups=mesh['row'=16,'col'=16] {'col'}, dimensions={0} | all-to-all | bytes 1664 | tf_op jit(solution)/shard_map/all_to_all | solution.py:19
  339.5 6.4 %all-to-all-start.7 = ((f32[16,1,13]{2,1,0:T(1,128)}), f32[16,1,13]{2,1,0:T(1,128)S(1)}, u32[]{:S(2)}, u32[]{:S(2)}) async-start(f32[16,1,13]{2,1,0:T(1,128)} %broadcast_in_dim.21), calls=%async_computation.7 | async-start | bytes 16384 | tf_op jit(solution)/shard_map/all_to_all | solution.py:19
  378.8 4.5 fusion.137
  388.7 6.0 %fusion.72 = (bf16[1024,1,4,64]{0,3,2,1:T(8,128)(2,1)S(1)}, bf16[1024,1,4,64]{0,3,2,1:T(8,128)(2,1)S(1)}) fusion(f32[]{:T(128)} %sqrt.15, f32[]{:T(128)} %bitcast.81, f32[1024,1,4,64]{0,3,2,1:T(8,128)} %copy.246, f32[]{:T(128)} %bitcast.80, f32[]{:T(128)} %sqrt.14, f32[1024,1,4,64]{0,3,2,1:T(8,128)S(1)} %copy.237, f32[]{:T(128)} %bitcast.35, f32[]{:T(128)} %bitcast.2, ...), kind=kLoop, calls=%fused_computation.141 | loop fusion | flops 8388608 | bytes 7340080 | tf_op jit(solution)/shard_map/convert
  417.3 26.5 %all-to-all-done.8 = f32[16,64,512]{2,1,0:T(8,128)S(1)} async-done(((f32[16,64,512]{2,1,0:T(8,128)}), f32[16,64,512]{2,1,0:T(8,128)S(1)}, u32[]{:S(2)}, u32[]{:S(2)}) %all-to-all-start.8) | async-done | bytes 2097184 | tf_op jit(solution)/shard_map/all_to_all | solution.py:71
  445.3 5.7 %stack.208 = f32[9]{0:T(128)S(1)} concatenate(f32[1]{0:T(128)} %bitcast.108, f32[1]{0:T(128)} %bitcast.109, f32[1]{0:T(128)} %bitcast.110, f32[1]{0:T(128)} %bitcast.111, f32[1]{0:T(128)} %bitcast.112, f32[1]{0:T(128)} %bitcast.113, f32[1]{0:T(128)} %bitcast.115, f32[1]{0:T(128)} %bitcast.116, f32[1]{0:T(128)} %bitcast.117), dimensions={0} | concatenate | bytes 72 | tf_op jit(solution)/shard_map/stack | solution.py:116
  451.0 10.3 %all_to_all.67 = f32[16,1,9]{2,1,0:T(1,128)S(1)} all-to-all(f32[16,1,9]{2,1,0:T(1,128)S(1)} %broadcast_in_dim.22), channel_id=1, replica_groups=mesh['row'=16,'col'=16] {'col'}, dimensions={0} | all-to-all | bytes 1152 | tf_op jit(solution)/shard_map/all_to_all | solution.py:19
  461.9 8.3 %all-to-all-start.10 = ((f32[16,1,9]{2,1,0:T(1,128)}), f32[16,1,9]{2,1,0:T(1,128)S(1)}, u32[]{:S(2)}, u32[]{:S(2)}) async-start(f32[16,1,9]{2,1,0:T(1,128)} %broadcast_in_dim.23), calls=%async_computation.10 | async-start | bytes 16384 | tf_op jit(solution)/shard_map/all_to_all | solution.py:19
  485.3 4.5 multiply_add_fusion
  (182 shorter events, 132.5 us)
Async XLA Ops:
  7.2 46.9 %all-gather.6.cloned.1.call-start = ((), (), s32[]{:S(2)}) async-start(), calls=%async_computation.11 | async-start | bytes 2228224 | tf_op jit(solution)/shard_map/all_gather | solution.py:83
  8.9 94.0 %all-gather.8.cloned.1.call-start = ((), (), s32[]{:S(2)}) async-start(), calls=%async_computation.12 | async-start | bytes 2228224 | tf_op jit(solution)/shard_map/all_gather | solution.py:47
  9.6 135.9 %all-gather.10.cloned.1.call-start = ((), (), s32[]{:S(2)}) async-start(), calls=%async_computation.13 | async-start | bytes 2228224 | tf_op jit(solution)/shard_map/all_gather | solution.py:48
  27.7 17.6 %all-to-all-start.1 = ((f32[16,1,2]{2,1,0:T(1,128)}), f32[16,1,2]{2,1,0:T(1,128)S(1)}, u32[]{:S(2)}, u32[]{:S(2)}) async-start(f32[16,1,2]{2,1,0:T(1,128)} %broadcast_in_dim.17), calls=%async_computation.1 | async-start | bytes 16384 | tf_op jit(solution)/shard_map/all_to_all | solution.py:19
  152.2 1.3 copy-start.6
  159.1 6.8 %copy-start = (bf16[64,4,64]{2,1,0:T(4,128)(2,1)S(1)}, bf16[64,4,64]{2,1,0:T(4,128)(2,1)}, u32[]{:S(2)}) copy-start(bf16[64,4,64]{2,1,0:T(4,128)(2,1)} %param.42) | copy-start | bytes 98308
  159.1 6.8 %copy-start.8 = (bf16[64,4,64]{2,1,0:T(4,128)(2,1)S(1)}, bf16[64,4,64]{2,1,0:T(4,128)(2,1)}, u32[]{:S(2)}) copy-start(bf16[64,4,64]{2,1,0:T(4,128)(2,1)} %param.43) | copy-start | bytes 98308
  159.1 36.0 %all-to-all-start.2 = ((f32[16,64,512]{2,1,0:T(8,128)}), f32[16,64,512]{2,1,0:T(8,128)}, u32[]{:S(2)}, u32[]{:S(2)}) async-start(f32[16,64,512]{2,1,0:T(8,128)} %bitcast.667), calls=%async_computation.2 | async-start | bytes 4194304 | tf_op jit(solution)/shard_map/all_to_all | solution.py:71
  165.8 31.2 %copy-start.9 = (f32[4]{0:T(128)S(1)}, f32[4]{0:T(128)}, u32[]{:S(2)}) copy-start(f32[4]{0:T(128)} %param.47) | copy-start | bytes 52
  165.8 75.6 %all-gather.12.cloned.1.call-start = ((), (), s32[]{:S(2)}) async-start(), calls=%async_computation.14 | async-start | bytes 4456448 | tf_op jit(solution)/shard_map/all_gather | solution.py:102
  252.9 1.6 copy-start.4
  277.6 33.8 %all-to-all-start.5 = ((f32[16,64,512]{2,1,0:T(8,128)}), f32[16,64,512]{2,1,0:T(8,128)}, u32[]{:S(2)}, u32[]{:S(2)}) async-start(f32[16,64,512]{2,1,0:T(8,128)} %bitcast.666), calls=%async_computation.5 | async-start | bytes 4194304 | tf_op jit(solution)/shard_map/all_to_all | solution.py:71
  282.1 96.8 %all-gather.14.cloned.1.call-start = ((), (), s32[]{:S(2)}) async-start(), calls=%async_computation.15 | async-start | bytes 4456448 | tf_op jit(solution)/shard_map/all_gather | solution.py:102
  316.7 0.7 copy-start.2
  339.5 13.5 %all-to-all-start.7 = ((f32[16,1,13]{2,1,0:T(1,128)}), f32[16,1,13]{2,1,0:T(1,128)S(1)}, u32[]{:S(2)}, u32[]{:S(2)}) async-start(f32[16,1,13]{2,1,0:T(1,128)} %broadcast_in_dim.21), calls=%async_computation.7 | async-start | bytes 16384 | tf_op jit(solution)/shard_map/all_to_all | solution.py:19
  349.8 0.6 copy-start.10
  394.7 1.6 copy-start.5
  401.8 3.4 copy-start.7
  410.7 3.9 copy-start.1
  410.7 3.9 copy-start.3
  410.7 33.0 %all-to-all-start.8 = ((f32[16,64,512]{2,1,0:T(8,128)}), f32[16,64,512]{2,1,0:T(8,128)S(1)}, u32[]{:S(2)}, u32[]{:S(2)}) async-start(f32[16,64,512]{2,1,0:T(8,128)} %bitcast.665), calls=%async_computation.8 | async-start | bytes 4194304 | tf_op jit(solution)/shard_map/all_to_all | solution.py:71
  417.3 60.2 %copy-start.11 = (f32[3,1]{0,1:T(1,128)S(1)}, f32[3,1]{0,1:T(1,128)}, u32[]{:S(2)}) copy-start(f32[3,1]{0,1:T(1,128)} %constant.468) | copy-start | bytes 40
  461.9 15.3 %all-to-all-start.10 = ((f32[16,1,9]{2,1,0:T(1,128)}), f32[16,1,9]{2,1,0:T(1,128)S(1)}, u32[]{:S(2)}, u32[]{:S(2)}) async-start(f32[16,1,9]{2,1,0:T(1,128)} %broadcast_in_dim.23), calls=%async_computation.10 | async-start | bytes 16384 | tf_op jit(solution)/shard_map/all_to_all | solution.py:19
Sparse Core Ops, SparseCore 0:
  10.4 43.6 all-gather.5
  56.5 46.3 all-gather.7
  104.7 40.7 all-gather.9
  198.0 40.0 all-gather.11
  318.2 38.6 all-gather.13

commit v7 on v6

--- a/solution.py
+++ b/solution.py
@@ -17,6 +17,12 @@
     size = lax.psum(1, axis)
     copies = jnp.broadcast_to(values[None], (size,) + values.shape)
     return jnp.sum(lax.all_to_all(copies, axis, 0, 0, tiled=False), axis=0)
+
+
+def gather_by_exchange(values, axis):
+    size = lax.psum(1, axis)
+    copies = jnp.broadcast_to(values[None], (size,) + values.shape)
+    return lax.all_to_all(copies, axis, 0, 0, tiled=False)
 
 
 def total(values):
@@ -44,7 +50,8 @@
 def local(site_tensor, site_tangent, left_env, right_env, mpo, dissipation):
     rows_here, physical, cols_here = site_tensor.shape
     channels = mpo.shape[0]
-    left_whole = lax.all_gather(left_env, "col", axis=1, tiled=True)
+    left_blocks = gather_by_exchange(left_env, "col")
+    left_whole = jnp.transpose(left_blocks, (1, 0, 2)).reshape(rows_here, -1)
     right_whole = lax.all_gather(right_env, "row", axis=0, tiled=True)
     right_whole = jnp.transpose(
         right_whole.reshape(right_whole.shape[0], cols_here, channels), (0, 2, 1)
@@ -80,9 +87,8 @@
     norm_tangent = starting[1] / norm_site
     basis = [primal / norm_site]
     tangents = [(tangent - basis[0] * norm_tangent) / norm_site]
-    inputs_whole = lax.all_gather(
-        jnp.stack([site_tensor, site_tangent], axis=1), "row", axis=0, tiled=True
-    ).astype(jnp.float32)
+    inputs_blocks = gather_by_exchange(jnp.stack([site_tensor, site_tangent], axis=1), "row")
+    inputs_whole = inputs_blocks.reshape((-1,) + inputs_blocks.shape[2:]).astype(jnp.float32)
     primal_whole = inputs_whole[:, 0]
     tangent_whole = inputs_whole[:, 1]
     basis_whole = [primal_whole / norm_site]

time: 499 us -> 495 us (level)
  starting transfers between devices: 40.6 us -> 57.6 us
  waiting for transfers between devices: 166 us -> 149 us
  blocking collectives: 59.8 us -> 45.4 us
  local copies, waits for them, and re-layouts: 118 us -> 129 us
    all_to_all x0 -> x2, waiting for transfers between devices: none -> 51.1 us  [gather_by_exchange(): return lax.all_to_all(copies, axis, 0, 0, tiled=False)]
    all_gather x2 -> x0, waiting for transfers between devices: 51 us -> none  [the longest x1 44.2 us: local(): left_whole = lax.all_gather(left_env, 'col', axis=1, tiled=True)]
    all_gather x1, waiting for transfers between devices: 19.1 us -> 0.02 us  [local(): right_whole = lax.all_gather(right_env, 'row', axis=0, tiled=True)]
    all_to_all x5 -> x4, blocking collectives: 59.8 us -> 45.4 us  [exchange_sum(): return jnp.sum(lax.all_to_all(copies, axis, 0, 0, tiled=False), axis=0)]
    all_to_all x0 -> x2, starting transfers between devices: none -> 8.83 us  [gather_by_exchange(): return lax.all_to_all(copies, axis, 0, 0, tiled=False)]
    all_to_all x3 -> x4, starting transfers between devices: 25.3 us -> 33.2 us  [exchange_sum(): return jnp.sum(lax.all_to_all(copies, axis, 0, 0, tiled=False), axis=0)]
    all_gather x2 -> x0, local copies, waits for them, and re-layouts: 7.7 us -> none  [the longest x1 4.78 us: local(): left_whole = lax.all_gather(left_env, 'col', axis=1, tiled=True)]
    convert_element_type x0 -> x2, local copies, waits for them, and re-layouts: none -> 6.65 us  [local(): inputs_blocks.reshape((-1,) + inputs_blocks.shape[2:]).astype(jnp.float32)]
  transfers between devices with their start and end apart: 11 -> 12, of which waited for: 9 -> 9; matrix products, arithmetic and copies ran while one was open for 17% -> 17% of each run, Pallas kernels for 0% -> 0%
where the time goes in v7:
time: 495 us; the launch traced here: 490 us
  waiting for transfers between devices  149 us (30%)
  local copies, waits for them, and re-layouts  129 us (26%)
  starting transfers between devices  57.6 us (12%)
  blocking collectives  45.4 us (9%)
  matrix products  37.6 us (8%)
  other arithmetic  36.2 us (7%)
  between operations  35 us (7%)
    all_to_all x3, waiting for transfers between devices, apply(): gathered = lax.all_to_all(split, 'col', 0, 0, tiled=False)  82.3 us
    all_to_all x2, waiting for transfers between devices, gather_by_exchange(): return lax.all_to_all(copies, axis, 0, 0, tiled=False)  51.1 us
    all_to_all x4, blocking collectives, exchange_sum(): return jnp.sum(lax.all_to_all(copies, axis, 0, 0, tiled=False), axis=0)  45.4 us
    all_to_all x4, starting transfers between devices, exchange_sum(): return jnp.sum(lax.all_to_all(copies, axis, 0, 0, tiled=False), axis=0)  33.2 us
    unnamed x38, local copies, waits for them, and re-layouts  21 us
    another operation x3, local copies, waits for them, and re-layouts, local(): totals = total(jnp.stack(locals_list))  18 us
    all_to_all x3, starting transfers between devices, apply(): gathered = lax.all_to_all(split, 'col', 0, 0, tiled=False)  15.2 us
    all_to_all x4, waiting for transfers between devices, exchange_sum(): return jnp.sum(lax.all_to_all(copies, axis, 0, 0, tiled=False), axis=0)  14.9 us
  transfers between devices with their start and end apart: 12, of which 9 were waited for; matrix products, arithmetic and copies ran while one was open for 17% of the time, Pallas kernels for 0%

profile of v7, /device:TPU:1, one launch (start us, length us, event | category | flops | bytes accessed | tf_op | source)
XLA Modules:
  0.0 489.6 jit_solution(13298426860948015073)
XLA Ops:
  10.7 7.6 %all-to-all-start = ((f32[16,1,2]{2,1,0:T(1,128)}), f32[16,1,2]{2,1,0:T(1,128)S(1)}, u32[]{:S(2)}, u32[]{:S(2)}) async-start(f32[16,1,2]{2,1,0:T(1,128)} %broadcast_in_dim.20), calls=%async_computation | async-start | bytes 16384 | tf_op jit(solution)/shard_map/all_to_all | solution.py:19
  19.4 5.2 %all-to-all-done = f32[16,1,2]{2,1,0:T(1,128)S(1)} async-done(((f32[16,1,2]{2,1,0:T(1,128)}), f32[16,1,2]{2,1,0:T(1,128)S(1)}, u32[]{:S(2)}, u32[]{:S(2)}) %all-to-all-start) | async-done | bytes 160 | tf_op jit(solution)/shard_map/all_to_all | solution.py:19
  25.3 10.6 %all-to-all-start.1 = ((f32[16,1,2]{2,1,0:T(1,128)}), f32[16,1,2]{2,1,0:T(1,128)S(1)}, u32[]{:S(2)}, u32[]{:S(2)}) async-start(f32[16,1,2]{2,1,0:T(1,128)} %broadcast_in_dim.21), calls=%async_computation.1 | async-start | bytes 16384 | tf_op jit(solution)/shard_map/all_to_all | solution.py:19
  38.7 4.2 all-to-all-done.1
  47.7 31.4 %all-to-all-done.2 = bf16[16,2,16384]{2,1,0:T(2,128)(2,1)S(1)} async-done(((bf16[16,2,16384]{2,1,0:T(2,128)(2,1)}), bf16[16,2,16384]{2,1,0:T(2,128)(2,1)S(1)}, u32[]{:S(2)}, u32[]{:S(2)}) %all-to-all-start.2) | async-done | bytes 1048608 | tf_op jit(solution)/shard_map/all_to_all | solution.py:25
  80.7 4.7 all-to-all-start.3
  95.6 19.8 %all-to-all-done.3 = bf16[16,64,1024]{2,1,0:T(8,128)(2,1)} async-done(((bf16[16,64,1024]{2,1,0:T(8,128)(2,1)}), bf16[16,64,1024]{2,1,0:T(8,128)(2,1)}, u32[]{:S(2)}, u32[]{:S(2)}) %all-to-all-start.3) | async-done | bytes 2097184 | tf_op jit(solution)/shard_map/all_to_all | solution.py:25
  115.3 4.8 copy.156
  120.1 5.5 %copy.158 = bf16[64,1024,16]{1,0,2:T(8,128)(2,1)} copy(bf16[64,1024,16]{0,2,1:T(8,128)(2,1)} %bitcast.670) | data formatting | bytes 4194304 | tf_op jit(solution)/shard_map/reshape;reshape | solution.py:64
  130.7 4.7 fusion.3
  152.2 6.9 %all-to-all-start.4 = ((f32[16,64,512]{2,1,0:T(8,128)}), f32[16,64,512]{2,1,0:T(8,128)}, u32[]{:S(2)}, u32[]{:S(2)}) async-start(f32[16,64,512]{2,1,0:T(8,128)} %bitcast.676), calls=%async_computation.4 | async-start | bytes 4194304 | tf_op jit(solution)/shard_map/all_to_all | solution.py:78
  159.5 28.9 %all-to-all-done.4 = f32[16,64,512]{2,1,0:T(8,128)} async-done(((f32[16,64,512]{2,1,0:T(8,128)}), f32[16,64,512]{2,1,0:T(8,128)}, u32[]{:S(2)}, u32[]{:S(2)}) %all-to-all-start.4) | async-done | bytes 2097184 | tf_op jit(solution)/shard_map/all_to_all | solution.py:78
  193.0 4.3 stack.176
  197.3 10.3 %all_to_all.73 = f32[16,1,7]{2,1,0:T(1,128)S(1)} all-to-all(f32[16,1,7]{2,1,0:T(1,128)S(1)} %broadcast_in_dim.24), channel_id=1, replica_groups=mesh['row'=16,'col'=16] {'col'}, dimensions={0} | all-to-all | bytes 896 | tf_op jit(solution)/shard_map/all_to_all | solution.py:19
  207.6 14.3 %all_to_all.74 = f32[16,1,7]{2,1,0:T(1,128)S(1)} all-to-all(f32[16,1,7]{2,1,0:T(1,128)S(1)} %broadcast_in_dim.25), channel_id=1, replica_groups=mesh['row'=16,'col'=16] {'row'}, dimensions={0} | all-to-all | bytes 896 | tf_op jit(solution)/shard_map/all_to_all | solution.py:19
  234.2 4.5 fusion.138
  249.5 4.7 reshape.632
  254.2 4.7 fusion.6
  258.8 4.1 reshape.633
  262.9 4.5 convolution_bitcast_fusion.1
  270.4 4.4 all-to-all-start.7
  277.1 27.0 %all-to-all-done.7 = f32[16,64,512]{2,1,0:T(8,128)} async-done(((f32[16,64,512]{2,1,0:T(8,128)}), f32[16,64,512]{2,1,0:T(8,128)}, u32[]{:S(2)}, u32[]{:S(2)}) %all-to-all-start.7) | async-done | bytes 2097184 | tf_op jit(solution)/shard_map/all_to_all | solution.py:78
  313.1 7.9 %stack.194 = f32[13]{0:T(128)S(1)} concatenate(f32[1]{0:T(128)} %bitcast.57, f32[1]{0:T(128)} %bitcast.58, f32[1]{0:T(128)} %bitcast.59, f32[1]{0:T(128)} %bitcast.60, f32[1]{0:T(128)} %bitcast.62, f32[1]{0:T(128)} %bitcast.63, f32[1]{0:T(128)} %bitcast.64, f32[1]{0:T(128)} %bitcast.65, f32[1]{0:T(128)} %bitcast.66, f32[1]{0:T(128)} %bitcast.67, f32[1]{0:T(128)} %bitcast.68, ...), dimensions={0} | concatenate | bytes 104 | tf_op jit(solution)/shard_map/stack | solution.py:122
  321.0 10.5 %all_to_all.75 = f32[16,1,13]{2,1,0:T(1,128)S(1)} all-to-all(f32[16,1,13]{2,1,0:T(1,128)S(1)} %broadcast_in_dim.26), channel_id=1, replica_groups=mesh['row'=16,'col'=16] {'col'}, dimensions={0} | all-to-all | bytes 1664 | tf_op jit(solution)/shard_map/all_to_all | solution.py:19
  332.2 6.4 %all-to-all-start.9 = ((f32[16,1,13]{2,1,0:T(1,128)}), f32[16,1,13]{2,1,0:T(1,128)S(1)}, u32[]{:S(2)}, u32[]{:S(2)}) async-start(f32[16,1,13]{2,1,0:T(1,128)} %broadcast_in_dim.27), calls=%async_computation.9 | async-start | bytes 16384 | tf_op jit(solution)/shard_map/all_to_all | solution.py:19
  371.4 4.5 fusion.137
  381.3 6.0 %fusion.72 = (bf16[1024,1,4,64]{0,3,2,1:T(8,128)(2,1)S(1)}, bf16[1024,1,4,64]{0,3,2,1:T(8,128)(2,1)S(1)}) fusion(f32[]{:T(128)} %sqrt.15, f32[]{:T(128)} %bitcast.82, f32[1024,1,4,64]{0,3,2,1:T(8,128)} %copy.249, f32[]{:T(128)} %bitcast.81, f32[]{:T(128)} %sqrt.14, f32[1024,1,4,64]{0,3,2,1:T(8,128)S(1)} %copy.240, f32[]{:T(128)} %bitcast.36, f32[]{:T(128)} %bitcast.2, ...), kind=kLoop, calls=%fused_computation.141 | loop fusion | flops 8388608 | bytes 7340080 | tf_op jit(solution)/shard_map/convert.1
  409.9 26.5 %all-to-all-done.10 = f32[16,64,512]{2,1,0:T(8,128)S(1)} async-done(((f32[16,64,512]{2,1,0:T(8,128)}), f32[16,64,512]{2,1,0:T(8,128)S(1)}, u32[]{:S(2)}, u32[]{:S(2)}) %all-to-all-start.10) | async-done | bytes 2097184 | tf_op jit(solution)/shard_map/all_to_all | solution.py:78
  437.8 5.7 %stack.208 = f32[9]{0:T(128)S(1)} concatenate(f32[1]{0:T(128)} %bitcast.109, f32[1]{0:T(128)} %bitcast.110, f32[1]{0:T(128)} %bitcast.111, f32[1]{0:T(128)} %bitcast.112, f32[1]{0:T(128)} %bitcast.113, f32[1]{0:T(128)} %bitcast.114, f32[1]{0:T(128)} %bitcast.116, f32[1]{0:T(128)} %bitcast.117, f32[1]{0:T(128)} %bitcast.118), dimensions={0} | concatenate | bytes 72 | tf_op jit(solution)/shard_map/stack | solution.py:122
  443.6 10.2 %all_to_all.76 = f32[16,1,9]{2,1,0:T(1,128)S(1)} all-to-all(f32[16,1,9]{2,1,0:T(1,128)S(1)} %broadcast_in_dim.28), channel_id=1, replica_groups=mesh['row'=16,'col'=16] {'col'}, dimensions={0} | all-to-all | bytes 1152 | tf_op jit(solution)/shard_map/all_to_all | solution.py:19
  454.4 8.7 %all-to-all-start.12 = ((f32[16,1,9]{2,1,0:T(1,128)}), f32[16,1,9]{2,1,0:T(1,128)S(1)}, u32[]{:S(2)}, u32[]{:S(2)}) async-start(f32[16,1,9]{2,1,0:T(1,128)} %broadcast_in_dim.29), calls=%async_computation.12 | async-start | bytes 16384 | tf_op jit(solution)/shard_map/all_to_all | solution.py:19
  478.1 4.5 multiply_add_fusion
  (192 shorter events, 146.6 us)
Async XLA Ops:
  10.7 13.9 %all-to-all-start = ((f32[16,1,2]{2,1,0:T(1,128)}), f32[16,1,2]{2,1,0:T(1,128)S(1)}, u32[]{:S(2)}, u32[]{:S(2)}) async-start(f32[16,1,2]{2,1,0:T(1,128)} %broadcast_in_dim.20), calls=%async_computation | async-start | bytes 16384 | tf_op jit(solution)/shard_map/all_to_all | solution.py:19
  25.3 17.6 %all-to-all-start.1 = ((f32[16,1,2]{2,1,0:T(1,128)}), f32[16,1,2]{2,1,0:T(1,128)S(1)}, u32[]{:S(2)}, u32[]{:S(2)}) async-start(f32[16,1,2]{2,1,0:T(1,128)} %broadcast_in_dim.21), calls=%async_computation.1 | async-start | bytes 16384 | tf_op jit(solution)/shard_map/all_to_all | solution.py:19
  36.4 42.6 %copy-start.10 = (bf16[64,1024]{1,0:T(8,128)(2,1)S(1)}, bf16[64,1024]{1,0:T(8,128)(2,1)}, u32[]{:S(2)}) copy-start(bf16[64,1024]{1,0:T(8,128)(2,1)} %param.44) | copy-start | bytes 393220
  42.8 36.2 %all-to-all-start.2 = ((bf16[16,2,16384]{2,1,0:T(2,128)(2,1)}), bf16[16,2,16384]{2,1,0:T(2,128)(2,1)S(1)}, u32[]{:S(2)}, u32[]{:S(2)}) async-start(bf16[16,2,16384]{2,1,0:T(2,128)(2,1)} %reshape.779), calls=%async_computation.2 | async-start | bytes 2097152 | tf_op jit(solution)/shard_map/all_to_all | solution.py:25
  46.9 91.6 %all-gather.4.cloned.1.call-start = ((), (), s32[]{:S(2)}) async-start(), calls=%async_computation.13 | async-start | bytes 2228224 | tf_op jit(solution)/shard_map/all_gather | solution.py:55
  80.7 4.7 copy-start.11
  80.7 34.7 %all-to-all-start.3 = ((bf16[16,64,1024]{2,1,0:T(8,128)(2,1)}), bf16[16,64,1024]{2,1,0:T(8,128)(2,1)}, u32[]{:S(2)}, u32[]{:S(2)}) async-start(bf16[16,64,1024]{2,1,0:T(8,128)(2,1)} %broadcast_in_dim.23), calls=%async_computation.3 | async-start | bytes 4194304 | tf_op jit(solution)/shard_map/all_to_all | solution.py:25
  125.6 1.6 copy-start.4
  145.3 1.3 copy-start.7
  152.2 7.2 %copy-start = (bf16[64,4,64]{2,1,0:T(4,128)(2,1)S(1)}, bf16[64,4,64]{2,1,0:T(4,128)(2,1)}, u32[]{:S(2)}) copy-start(bf16[64,4,64]{2,1,0:T(4,128)(2,1)} %param.42) | copy-start | bytes 98308
  152.2 7.2 %copy-start.9 = (bf16[64,4,64]{2,1,0:T(4,128)(2,1)S(1)}, bf16[64,4,64]{2,1,0:T(4,128)(2,1)}, u32[]{:S(2)}) copy-start(bf16[64,4,64]{2,1,0:T(4,128)(2,1)} %param.43) | copy-start | bytes 98308
  152.2 36.2 %all-to-all-start.4 = ((f32[16,64,512]{2,1,0:T(8,128)}), f32[16,64,512]{2,1,0:T(8,128)}, u32[]{:S(2)}, u32[]{:S(2)}) async-start(f32[16,64,512]{2,1,0:T(8,128)} %bitcast.676), calls=%async_computation.4 | async-start | bytes 4194304 | tf_op jit(solution)/shard_map/all_to_all | solution.py:78
  159.1 31.1 %copy-start.12 = (f32[4]{0:T(128)S(1)}, f32[4]{0:T(128)}, u32[]{:S(2)}) copy-start(f32[4]{0:T(128)} %param.47) | copy-start | bytes 52
  159.1 75.0 %all-gather.6.cloned.1.call-start = ((), (), s32[]{:S(2)}) async-start(), calls=%async_computation.14 | async-start | bytes 4456448 | tf_op jit(solution)/shard_map/all_gather | solution.py:108
  245.6 1.6 copy-start.5
  270.4 33.8 %all-to-all-start.7 = ((f32[16,64,512]{2,1,0:T(8,128)}), f32[16,64,512]{2,1,0:T(8,128)}, u32[]{:S(2)}, u32[]{:S(2)}) async-start(f32[16,64,512]{2,1,0:T(8,128)} %bitcast.675), calls=%async_computation.7 | async-start | bytes 4194304 | tf_op jit(solution)/shard_map/all_to_all | solution.py:78
  274.8 96.6 %all-gather.8.cloned.1.call-start = ((), (), s32[]{:S(2)}) async-start(), calls=%async_computation.15 | async-start | bytes 4456448 | tf_op jit(solution)/shard_map/all_gather | solution.py:108
  309.4 0.7 copy-start.2
  332.2 13.5 %all-to-all-start.9 = ((f32[16,1,13]{2,1,0:T(1,128)}), f32[16,1,13]{2,1,0:T(1,128)S(1)}, u32[]{:S(2)}, u32[]{:S(2)}) async-start(f32[16,1,13]{2,1,0:T(1,128)} %broadcast_in_dim.27), calls=%async_computation.9 | async-start | bytes 16384 | tf_op jit(solution)/shard_map/all_to_all | solution.py:19
  342.8 0.6 copy-start.13
  387.3 1.6 copy-start.6
  394.4 3.4 copy-start.8
  403.3 3.9 copy-start.1
  403.3 3.9 copy-start.3
  403.3 33.0 %all-to-all-start.10 = ((f32[16,64,512]{2,1,0:T(8,128)}), f32[16,64,512]{2,1,0:T(8,128)S(1)}, u32[]{:S(2)}, u32[]{:S(2)}) async-start(f32[16,64,512]{2,1,0:T(8,128)} %bitcast.674), calls=%async_computation.10 | async-start | bytes 4194304 | tf_op jit(solution)/shard_map/all_to_all | solution.py:78
  409.9 60.5 %copy-start.14 = (f32[3,1]{0,1:T(1,128)S(1)}, f32[3,1]{0,1:T(1,128)}, u32[]{:S(2)}) copy-start(f32[3,1]{0,1:T(1,128)} %constant.468) | copy-start | bytes 40
  454.4 15.6 %all-to-all-start.12 = ((f32[16,1,9]{2,1,0:T(1,128)}), f32[16,1,9]{2,1,0:T(1,128)S(1)}, u32[]{:S(2)}, u32[]{:S(2)}) async-start(f32[16,1,9]{2,1,0:T(1,128)} %broadcast_in_dim.29), calls=%async_computation.12 | async-start | bytes 16384 | tf_op jit(solution)/shard_map/all_to_all | solution.py:19
Sparse Core Ops, SparseCore 0:
  49.6 43.1 all-gather.3
  191.2 39.4 all-gather.5
  311.0 38.5 all-gather.7

commit v8 on v7

--- a/solution.py
+++ b/solution.py
@@ -87,8 +87,9 @@
     norm_tangent = starting[1] / norm_site
     basis = [primal / norm_site]
     tangents = [(tangent - basis[0] * norm_tangent) / norm_site]
-    inputs_blocks = gather_by_exchange(jnp.stack([site_tensor, site_tangent], axis=1), "row")
-    inputs_whole = inputs_blocks.reshape((-1,) + inputs_blocks.shape[2:]).astype(jnp.float32)
+    inputs_whole = lax.all_gather(
+        jnp.stack([site_tensor, site_tangent], axis=1), "row", axis=0, tiled=True
+    ).astype(jnp.float32)
     primal_whole = inputs_whole[:, 0]
     tangent_whole = inputs_whole[:, 1]
     basis_whole = [primal_whole / norm_site]

time: 495 us -> 453 us (0.915)
  waiting for transfers between devices: 149 us -> 110 us
  blocking collectives: 45.4 us -> 79.1 us
  starting transfers between devices: 57.6 us -> 32.1 us
  local copies, waits for them, and re-layouts: 129 us -> 120 us
    all_to_all x4 -> x6, blocking collectives: 45.4 us -> 79.1 us  [exchange_sum(): return jnp.sum(lax.all_to_all(copies, axis, 0, 0, tiled=False), axis=0)]
    all_to_all x2 -> x1, waiting for transfers between devices: 51.1 us -> 23.1 us  [gather_by_exchange(): return lax.all_to_all(copies, axis, 0, 0, tiled=False)]
    all_to_all x4 -> x2, starting transfers between devices: 33.2 us -> 14.5 us  [exchange_sum(): return jnp.sum(lax.all_to_all(copies, axis, 0, 0, tiled=False), axis=0)]
    all_to_all x4 -> x2, waiting for transfers between devices: 14.9 us -> 5.7 us  [exchange_sum(): return jnp.sum(lax.all_to_all(copies, axis, 0, 0, tiled=False), axis=0)]
    convert_element_type x2 -> x0, local copies, waits for them, and re-layouts: 6.65 us -> none  [local(): inputs_blocks.reshape((-1,) + inputs_blocks.shape[2:]).astype(jnp.float32)]
    unnamed x38 -> x33, local copies, waits for them, and re-layouts: 21 us -> 16.9 us
  transfers between devices with their start and end apart: 12 -> 10, of which waited for: 9 -> 7; matrix products, arithmetic and copies ran while one was open for 17% -> 18% of each run, Pallas kernels for 0% -> 0%
where the time goes in v8:
time: 453 us; the launch traced here: 450 us
  local copies, waits for them, and re-layouts  120 us (26%)
  waiting for transfers between devices  110 us (24%)
  blocking collectives  79.1 us (17%)
  matrix products  37.7 us (8%)
  other arithmetic  37.1 us (8%)
  between operations  34.4 us (8%)
  starting transfers between devices  32.1 us (7%)
    all_to_all x6, blocking collectives, exchange_sum(): return jnp.sum(lax.all_to_all(copies, axis, 0, 0, tiled=False), axis=0)  79.1 us
    all_to_all x3, waiting for transfers between devices, apply(): gathered = lax.all_to_all(split, 'col', 0, 0, tiled=False)  79.1 us
    all_to_all x1, waiting for transfers between devices, gather_by_exchange(): return lax.all_to_all(copies, axis, 0, 0, tiled=False)  23.1 us
    another operation x3, local copies, waits for them, and re-layouts, local(): totals = total(jnp.stack(locals_list))  18 us
    unnamed x33, local copies, waits for them, and re-layouts  16.9 us
    all_to_all x2, starting transfers between devices, exchange_sum(): return jnp.sum(lax.all_to_all(copies, axis, 0, 0, tiled=False), axis=0)  14.5 us
    all_to_all x3, starting transfers between devices, apply(): gathered = lax.all_to_all(split, 'col', 0, 0, tiled=False)  12.9 us
    dot_general x3, matrix products, apply(): jnp.einsum('awspr,wvpq->asqvr', mixed, mpo, preferred_element_type=jnp.fl...  12.5 us
  transfers between devices with their start and end apart: 10, of which 7 were waited for; matrix products, arithmetic and copies ran while one was open for 18% of the time, Pallas kernels for 0%

profile of v8, /device:TPU:1, one launch (start us, length us, event | category | flops | bytes accessed | tf_op | source)
XLA Modules:
  0.0 450.2 jit_solution(12404494416778529956)
XLA Ops:
  12.6 13.8 %all_to_all.68 = f32[16,1,2]{2,1,0:T(1,128)S(1)} all-to-all(f32[16,1,2]{2,1,0:T(1,128)S(1)} %broadcast_in_dim.18), channel_id=1, replica_groups=mesh['row'=16,'col'=16] {'col'}, dimensions={0} | all-to-all | bytes 256 | tf_op jit(solution)/shard_map/all_to_all | solution.py:19
  26.4 17.4 %all_to_all.69 = f32[16,1,2]{2,1,0:T(1,128)S(1)} all-to-all(f32[16,1,2]{2,1,0:T(1,128)S(1)} %broadcast_in_dim.19), channel_id=1, replica_groups=mesh['row'=16,'col'=16] {'row'}, dimensions={0} | all-to-all | bytes 256 | tf_op jit(solution)/shard_map/all_to_all | solution.py:19
  46.3 4.6 %all-to-all-start.2 = ((bf16[16,64,1024]{2,1,0:T(8,128)(2,1)}), bf16[16,64,1024]{2,1,0:T(8,128)(2,1)}, u32[]{:S(2)}, u32[]{:S(2)}) async-start(bf16[16,64,1024]{2,1,0:T(8,128)(2,1)} %broadcast_in_dim.20), calls=%async_computation.2 | async-start | bytes 4194304 | tf_op jit(solution)/shard_map/all_to_all | solution.py:25
  57.0 23.1 %all-to-all-done.2 = bf16[16,64,1024]{2,1,0:T(8,128)(2,1)} async-done(((bf16[16,64,1024]{2,1,0:T(8,128)(2,1)}), bf16[16,64,1024]{2,1,0:T(8,128)(2,1)}, u32[]{:S(2)}, u32[]{:S(2)}) %all-to-all-start.2) | async-done | bytes 2097184 | tf_op jit(solution)/shard_map/all_to_all | solution.py:25
  80.1 4.8 %copy.153 = bf16[64,16,1024]{0,2,1:T(8,128)(2,1)} copy(bf16[64,16,1024]{2,0,1:T(8,128)(2,1)} %bitcast.8) | data formatting | bytes 4194304 | tf_op jit(solution)/shard_map/transpose | solution.py:54
  84.9 5.5 %copy.155 = bf16[64,1024,16]{1,0,2:T(8,128)(2,1)} copy(bf16[64,1024,16]{0,2,1:T(8,128)(2,1)} %bitcast.663) | data formatting | bytes 4194304 | tf_op jit(solution)/shard_map/reshape;reshape | solution.py:64
  95.5 4.7 %fusion.3 = bf16[64,2,4,16,64]{4,3,2,1,0:T(8,128)(2,1)} fusion(bf16[16,16,4,4,1,1]{0,1,2,3,5,4:T(8,128)(2,1)S(1)} %copy.192, bf16[64,16,2,4,64,1]{4,3,2,0,1,5:T(4,128)(2,1)} %bitcast.681), kind=kOutput, calls=%fused_computation.6 | convolution fusion | flops 67633152 | bytes 2105344 | tf_op jit(solution)/shard_map/awspr,wvpq->asqvr/dot_general | solution.py:69
  103.4 4.0 copy.158
  117.0 4.6 %all-to-all-start.3 = ((f32[16,64,512]{2,1,0:T(8,128)}), f32[16,64,512]{2,1,0:T(8,128)}, u32[]{:S(2)}, u32[]{:S(2)}) async-start(f32[16,64,512]{2,1,0:T(8,128)} %bitcast.668), calls=%async_computation.3 | async-start | bytes 4194304 | tf_op jit(solution)/shard_map/all_to_all | solution.py:78
  121.7 25.5 %all-to-all-done.3 = f32[16,64,512]{2,1,0:T(8,128)} async-done(((f32[16,64,512]{2,1,0:T(8,128)}), f32[16,64,512]{2,1,0:T(8,128)}, u32[]{:S(2)}, u32[]{:S(2)}) %all-to-all-start.3) | async-done | bytes 2097184 | tf_op jit(solution)/shard_map/all_to_all | solution.py:78
  151.8 4.3 stack.176
  156.2 11.9 %all_to_all.70 = f32[16,1,7]{2,1,0:T(1,128)S(1)} all-to-all(f32[16,1,7]{2,1,0:T(1,128)S(1)} %broadcast_in_dim.21), channel_id=1, replica_groups=mesh['row'=16,'col'=16] {'col'}, dimensions={0} | all-to-all | bytes 896 | tf_op jit(solution)/shard_map/all_to_all | solution.py:19
  168.1 14.9 %all_to_all.71 = f32[16,1,7]{2,1,0:T(1,128)S(1)} all-to-all(f32[16,1,7]{2,1,0:T(1,128)S(1)} %broadcast_in_dim.22), channel_id=1, replica_groups=mesh['row'=16,'col'=16] {'row'}, dimensions={0} | all-to-all | bytes 896 | tf_op jit(solution)/shard_map/all_to_all | solution.py:19
  195.2 4.5 %fusion.138 = (f32[1024,1,4,64]{3,2,1,0:T(4,128)}, f32[1024,1,4,64]{3,2,1,0:T(4,128)}) fusion(f32[1024,2,4,64]{3,2,1,0:T(4,128)} %all-gather.9.cloned.1.call-done), kind=kLoop, calls=%fused_computation.264 | loop fusion | bytes 4194304 | tf_op jit(solution)/shard_map/slice | solution.py:110
  210.6 4.7 %reshape.628 = bf16[64,16,2,4,64]{4,3,2,0,1:T(4,128)(2,1)} reshape(bf16[64,16,512]{2,0,1:T(8,128)(2,1)} %fusion.13) | data formatting | bytes 2097152 | tf_op jit(solution)/shard_map/reshape | solution.py:68
  215.2 4.7 %fusion.6 = bf16[64,2,4,16,64]{4,3,2,1,0:T(8,128)(2,1)} fusion(bf16[16,16,4,4,1,1]{0,1,2,3,5,4:T(8,128)(2,1)S(1)} %copy.192, bf16[64,16,2,4,64,1]{4,3,2,0,1,5:T(4,128)(2,1)} %bitcast.682), kind=kOutput, calls=%fused_computation.7 | convolution fusion | flops 67633152 | bytes 2105344 | tf_op jit(solution)/shard_map/awspr,wvpq->asqvr/dot_general | solution.py:69
  219.9 4.1 reshape.629
  224.0 4.5 convolution_bitcast_fusion.1
  231.4 4.4 all-to-all-start.6
  238.2 27.0 %all-to-all-done.6 = f32[16,64,512]{2,1,0:T(8,128)} async-done(((f32[16,64,512]{2,1,0:T(8,128)}), f32[16,64,512]{2,1,0:T(8,128)}, u32[]{:S(2)}, u32[]{:S(2)}) %all-to-all-start.6) | async-done | bytes 2097184 | tf_op jit(solution)/shard_map/all_to_all | solution.py:78
  274.1 7.9 %stack.194 = f32[13]{0:T(128)S(1)} concatenate(f32[1]{0:T(128)} %bitcast.57, f32[1]{0:T(128)} %bitcast.58, f32[1]{0:T(128)} %bitcast.59, f32[1]{0:T(128)} %bitcast.60, f32[1]{0:T(128)} %bitcast.62, f32[1]{0:T(128)} %bitcast.63, f32[1]{0:T(128)} %bitcast.64, f32[1]{0:T(128)} %bitcast.65, f32[1]{0:T(128)} %bitcast.66, f32[1]{0:T(128)} %bitcast.67, f32[1]{0:T(128)} %bitcast.68, ...), dimensions={0} | concatenate | bytes 104 | tf_op jit(solution)/shard_map/stack | solution.py:123
  282.1 10.5 %all_to_all.72 = f32[16,1,13]{2,1,0:T(1,128)S(1)} all-to-all(f32[16,1,13]{2,1,0:T(1,128)S(1)} %broadcast_in_dim.23), channel_id=1, replica_groups=mesh['row'=16,'col'=16] {'col'}, dimensions={0} | all-to-all | bytes 1664 | tf_op jit(solution)/shard_map/all_to_all | solution.py:19
  293.2 6.6 %all-to-all-start.8 = ((f32[16,1,13]{2,1,0:T(1,128)}), f32[16,1,13]{2,1,0:T(1,128)S(1)}, u32[]{:S(2)}, u32[]{:S(2)}) async-start(f32[16,1,13]{2,1,0:T(1,128)} %broadcast_in_dim.24), calls=%async_computation.8 | async-start | bytes 16384 | tf_op jit(solution)/shard_map/all_to_all | solution.py:19
  332.7 4.5 %fusion.137 = (f32[1024,1,4,64]{3,2,1,0:T(4,128)}, f32[1024,1,4,64]{3,2,1,0:T(4,128)}) fusion(f32[1024,2,4,64]{3,2,1,0:T(4,128)} %all-gather.11.cloned.1.call-done), kind=kLoop, calls=%fused_computation.263 | loop fusion | bytes 4194304 | tf_op jit(solution)/shard_map/slice | solution.py:110
  342.7 6.0 %fusion.72 = (bf16[1024,1,4,64]{0,3,2,1:T(8,128)(2,1)S(1)}, bf16[1024,1,4,64]{0,3,2,1:T(8,128)(2,1)S(1)}) fusion(f32[]{:T(128)} %sqrt.15, f32[]{:T(128)} %bitcast.82, f32[1024,1,4,64]{0,3,2,1:T(8,128)} %copy.246, f32[]{:T(128)} %bitcast.81, f32[]{:T(128)} %sqrt.14, f32[1024,1,4,64]{0,3,2,1:T(8,128)S(1)} %copy.237, f32[]{:T(128)} %bitcast.36, f32[]{:T(128)} %bitcast.2, ...), kind=kLoop, calls=%fused_computation.141 | loop fusion | flops 8388608 | bytes 7340080 | tf_op jit(solution)/shard_map/convert
  355.8 3.4 reshape.642
  364.7 3.8 all-to-all-start.9
  371.3 26.6 %all-to-all-done.9 = f32[16,64,512]{2,1,0:T(8,128)S(1)} async-done(((f32[16,64,512]{2,1,0:T(8,128)}), f32[16,64,512]{2,1,0:T(8,128)S(1)}, u32[]{:S(2)}, u32[]{:S(2)}) %all-to-all-start.9) | async-done | bytes 2097184 | tf_op jit(solution)/shard_map/all_to_all | solution.py:78
  399.3 5.7 %stack.208 = f32[9]{0:T(128)S(1)} concatenate(f32[1]{0:T(128)} %bitcast.109, f32[1]{0:T(128)} %bitcast.110, f32[1]{0:T(128)} %bitcast.111, f32[1]{0:T(128)} %bitcast.112, f32[1]{0:T(128)} %bitcast.113, f32[1]{0:T(128)} %bitcast.114, f32[1]{0:T(128)} %bitcast.116, f32[1]{0:T(128)} %bitcast.117, f32[1]{0:T(128)} %bitcast.118), dimensions={0} | concatenate | bytes 72 | tf_op jit(solution)/shard_map/stack | solution.py:123
  405.0 10.6 %all_to_all.73 = f32[16,1,9]{2,1,0:T(1,128)S(1)} all-to-all(f32[16,1,9]{2,1,0:T(1,128)S(1)} %broadcast_in_dim.25), channel_id=1, replica_groups=mesh['row'=16,'col'=16] {'col'}, dimensions={0} | all-to-all | bytes 1152 | tf_op jit(solution)/shard_map/all_to_all | solution.py:19
  416.3 7.9 %all-to-all-start.11 = ((f32[16,1,9]{2,1,0:T(1,128)}), f32[16,1,9]{2,1,0:T(1,128)S(1)}, u32[]{:S(2)}, u32[]{:S(2)}) async-start(f32[16,1,9]{2,1,0:T(1,128)} %broadcast_in_dim.26), calls=%async_computation.11 | async-start | bytes 16384 | tf_op jit(solution)/shard_map/all_to_all | solution.py:19
  439.2 4.5 %multiply_add_fusion = (f32[32,8,64]{2,1,0:T(8,128)}, f32[32,8,64]{2,1,0:T(8,128)}) fusion(f32[32,8,64]{2,1,0:T(8,128)S(1)} %bitcast.679, f32[32,8,64]{2,1,0:T(8,128)S(1)} %bitcast.677, f32[32,8,64]{2,1,0:T(8,128)S(1)} %bitcast.675, f32[32,8,64]{2,1,0:T(8,128)S(1)} %bitcast.673, f32[32,8,64]{2,1,0:T(8,128)S(1)} %bitcast.665, f32[]{:T(128)} %bitcast.225, ...), kind=kLoop, calls=%fused_computation.153 | loop fusion | flops 360448 | bytes 491552 | tf_op jit(solution)/shard_map/add | solution.py:189
  (185 shorter events, 124.8 us)
Async XLA Ops:
  7.2 46.7 %all-gather.5.cloned.1.call-start = ((), (), s32[]{:S(2)}) async-start(), calls=%async_computation.12 | async-start | bytes 2228224 | tf_op jit(solution)/shard_map/all_gather | solution.py:90
  8.9 94.5 %all-gather.7.cloned.1.call-start = ((), (), s32[]{:S(2)}) async-start(), calls=%async_computation.13 | async-start | bytes 2228224 | tf_op jit(solution)/shard_map/all_gather | solution.py:55
  46.3 4.6 %copy-start.10 = (bf16[16,16,4,4]{1,3,2,0:T(4,128)(2,1)S(1)}, bf16[16,16,4,4]{1,3,2,0:T(4,128)(2,1)}, u32[]{:S(2)}) copy-start(bf16[16,16,4,4]{1,3,2,0:T(4,128)(2,1)} %param.46) | copy-start | bytes 24580
  46.3 33.8 %all-to-all-start.2 = ((bf16[16,64,1024]{2,1,0:T(8,128)(2,1)}), bf16[16,64,1024]{2,1,0:T(8,128)(2,1)}, u32[]{:S(2)}, u32[]{:S(2)}) async-start(bf16[16,64,1024]{2,1,0:T(8,128)(2,1)} %broadcast_in_dim.20), calls=%async_computation.2 | async-start | bytes 4194304 | tf_op jit(solution)/shard_map/all_to_all | solution.py:25
  90.5 1.6 copy-start.4
  110.1 1.3 copy-start.7
  117.0 4.6 %copy-start = (bf16[64,4,64]{2,1,0:T(4,128)(2,1)S(1)}, bf16[64,4,64]{2,1,0:T(4,128)(2,1)}, u32[]{:S(2)}) copy-start(bf16[64,4,64]{2,1,0:T(4,128)(2,1)} %param.42) | copy-start | bytes 98308
  117.0 4.7 %copy-start.9 = (bf16[64,4,64]{2,1,0:T(4,128)(2,1)S(1)}, bf16[64,4,64]{2,1,0:T(4,128)(2,1)}, u32[]{:S(2)}) copy-start(bf16[64,4,64]{2,1,0:T(4,128)(2,1)} %param.43) | copy-start | bytes 98308
  117.0 30.3 %all-to-all-start.3 = ((f32[16,64,512]{2,1,0:T(8,128)}), f32[16,64,512]{2,1,0:T(8,128)}, u32[]{:S(2)}, u32[]{:S(2)}) async-start(f32[16,64,512]{2,1,0:T(8,128)} %bitcast.668), calls=%async_computation.3 | async-start | bytes 4194304 | tf_op jit(solution)/shard_map/all_to_all | solution.py:78
  121.5 27.6 %copy-start.11 = (f32[4]{0:T(128)S(1)}, f32[4]{0:T(128)}, u32[]{:S(2)}) copy-start(f32[4]{0:T(128)} %param.47) | copy-start | bytes 52
  121.6 73.6 %all-gather.9.cloned.1.call-start = ((), (), s32[]{:S(2)}) async-start(), calls=%async_computation.14 | async-start | bytes 4456448 | tf_op jit(solution)/shard_map/all_gather | solution.py:109
  206.7 1.6 copy-start.5
  231.4 33.8 %all-to-all-start.6 = ((f32[16,64,512]{2,1,0:T(8,128)}), f32[16,64,512]{2,1,0:T(8,128)}, u32[]{:S(2)}, u32[]{:S(2)}) async-start(f32[16,64,512]{2,1,0:T(8,128)} %bitcast.667), calls=%async_computation.6 | async-start | bytes 4194304 | tf_op jit(solution)/shard_map/all_to_all | solution.py:78
  235.9 96.9 %all-gather.11.cloned.1.call-start = ((), (), s32[]{:S(2)}) async-start(), calls=%async_computation.15 | async-start | bytes 4456448 | tf_op jit(solution)/shard_map/all_gather | solution.py:109
  270.4 0.7 copy-start.2
  293.2 13.6 %all-to-all-start.8 = ((f32[16,1,13]{2,1,0:T(1,128)}), f32[16,1,13]{2,1,0:T(1,128)S(1)}, u32[]{:S(2)}, u32[]{:S(2)}) async-start(f32[16,1,13]{2,1,0:T(1,128)} %broadcast_in_dim.24), calls=%async_computation.8 | async-start | bytes 16384 | tf_op jit(solution)/shard_map/all_to_all | solution.py:19
  303.8 0.6 copy-start.12
  348.6 1.6 copy-start.6
  355.8 3.4 copy-start.8
  364.7 3.9 copy-start.1
  364.7 3.9 copy-start.3
  364.7 33.2 %all-to-all-start.9 = ((f32[16,64,512]{2,1,0:T(8,128)}), f32[16,64,512]{2,1,0:T(8,128)S(1)}, u32[]{:S(2)}, u32[]{:S(2)}) async-start(f32[16,64,512]{2,1,0:T(8,128)} %bitcast.666), calls=%async_computation.9 | async-start | bytes 4194304 | tf_op jit(solution)/shard_map/all_to_all | solution.py:78
  371.2 60.2 %copy-start.13 = (f32[3,1]{0,1:T(1,128)S(1)}, f32[3,1]{0,1:T(1,128)}, u32[]{:S(2)}) copy-start(f32[3,1]{0,1:T(1,128)} %constant.468) | copy-start | bytes 40
  416.3 14.9 %all-to-all-start.11 = ((f32[16,1,9]{2,1,0:T(1,128)}), f32[16,1,9]{2,1,0:T(1,128)S(1)}, u32[]{:S(2)}, u32[]{:S(2)}) async-start(f32[16,1,9]{2,1,0:T(1,128)} %broadcast_in_dim.26), calls=%async_computation.11 | async-start | bytes 16384 | tf_op jit(solution)/shard_map/all_to_all | solution.py:19
Sparse Core Ops, SparseCore 0:
  10.4 43.4 all-gather.4
  55.7 37.9 all-gather.6
  150.1 41.7 all-gather.8
  272.0 38.9 all-gather.10
